TPU v7x, 256 devices: a whole 4x4x8 slice. The times are simulated.
256 devices in a mesh: seq: 32 (over z, x), tp: 8 (over y, core).
Axes of the slice: x: 4, y: 4, z: 8, core: 2. Of those that a mesh axis runs over, the one named last changes fastest.
Arguments:
- prefill_states: bfloat16 [8192, 1536], P('seq'), may hold values from -6 to 6
- decode_states: bfloat16 [256, 1536], P(('seq', 'tp')), may hold values from -6 to 6
- attn_gain: bfloat16 [1536], replicated, may hold values from 0.25 to 1.75
- query_weight: bfloat16 [1536, 1536], P(None, 'tp'), may hold values from -0.625 to 0.625
- keyvalue_weight: bfloat16 [1536, 8, 128], P(None, 'tp'), as said below
- output_weight: bfloat16 [1536, 1536], P('tp'), may hold values from -0.3125 to 0.3125
- cache_keyval: bfloat16 [256, 2048, 8, 128], P(None, 'seq', 'tp'), may hold values from -68 to 68, as said below
- cached_length: int32 [256], replicated, may hold values from 1 to 2048, as said below
- span_tenant: int32 [4], replicated, may hold values from 0 to 3
- ffn_gain: bfloat16 [1536], replicated, may hold values from 0.25 to 1.75
- expert_in: bfloat16 [32, 1536, 1024], P('seq'), may hold values from -0.15625 to 0.15625
- expert_out: bfloat16 [32, 512, 1536], P('seq'), may hold values from -0.25 to 0.25
- routes: int32 [8448, 8], P(('seq', 'tp')), may hold values from 0 to 31, all different within a row; in each aligned block of 33 rows (0 to 32, 33 to 65, ...) at most 18 rows name the same one
- gate_values: float32 [8448, 8], P(('seq', 'tp')), may hold values from 0.05 to 0.3
Outputs:
- prefill_out: bfloat16 [8192, 1536], P(('seq', 'tp'))
- decode_out: bfloat16 [256, 1536], P(('seq', 'tp'))
Inputs may be any that keep to these rules, and one draw needn't show every extreme that they name: `cached_length`: positions at or beyond a request's length hold no key; the new token stands at that length. `cache_keyval`: keys are rotated at their positions. `keyvalue_weight`: keys first, then values, in each head. `routes`: in the rows of one device no expert is named more than 18 times, a bound that some block reaches.
All inputs are finite; a program needn't handle non-finite values.
Results may differ from a plain program's by a relative error of at most 0.02.
The roundings to bfloat16 on the way count: a program that leaves them out, or rounds other values in their place, can miss the bound.
Values may be sent and summed in bfloat16 or wider, within the bound.
No kernel may reach another device: no remote copies, remote signals or barrier semaphores. Data moves between devices by JAX's collectives and lax.ppermute only.
A program may use at most 128 MiB of HBM per device.

v0:
```python
import math

import jax
import jax.numpy as jnp
from jax import lax
from jax.sharding import PartitionSpec as P

EXPERTS = 32
SPAN = 2048


eps_norm = 1e-05
rope_base = 10000.0
masked_score = -1e30
key_block = 512


def rms_norm(values, scales):
    floats = values.astype(jnp.float32)
    factor = lax.rsqrt(jnp.mean(floats * floats, axis=-1, keepdims=True) + eps_norm)
    return (floats * factor * scales.astype(jnp.float32)).astype(jnp.bfloat16)


def apply_rotary(values, token_positions):
    half_dim = values.shape[-1] // 2
    frequency = rope_base ** (-2.0 * jnp.arange(half_dim, dtype=jnp.float32) / values.shape[-1])
    angles = token_positions.astype(jnp.float32)[:, None] * frequency[None, :]
    cosine = jnp.cos(angles)[:, None, :]
    sine_part = jnp.sin(angles)[:, None, :]
    first_half = values[..., :half_dim]
    second_half = values[..., half_dim:]
    return jnp.concatenate(
        [
            first_half * cosine - second_half * sine_part,
            second_half * cosine + first_half * sine_part,
        ],
        axis=-1,
    )


def span_tables(span_tenant):
    span_count = span_tenant.shape[0]
    ordinal = jnp.arange(span_count, dtype=jnp.int32)
    same_tenant = span_tenant[:, None] == span_tenant[None, :]
    earlier = ordinal[None, :] < ordinal[:, None]
    return jnp.sum(jnp.where(same_tenant & earlier, 1, 0), axis=1).astype(jnp.int32)


def token_tables(token_index, span_tenant, before):
    span_count = span_tenant.shape[0]
    span_index = token_index // SPAN
    onehot = span_index[:, None] == jnp.arange(span_count, dtype=jnp.int32)[None, :]
    tenant = jnp.sum(jnp.where(onehot, span_tenant[None, :], 0), axis=1)
    offset = jnp.sum(jnp.where(onehot, before[None, :], 0), axis=1)
    return (tenant, offset * SPAN + token_index % SPAN)


def attend_keys(fold_state, keyvalue_rows, visible, query_matrix, score_scale):
    run_max, run_total, run_acc = fold_state
    head_dim = keyvalue_rows.shape[-1] // 2
    scores = (
        jnp.einsum(
            "qhgd,khd->qhgk",
            query_matrix,
            keyvalue_rows[..., :head_dim],
            preferred_element_type=jnp.float32,
        )
        * score_scale
    )
    mask_full = visible[:, None, None, :]
    scores = jnp.where(mask_full, scores, masked_score)
    new_max = jnp.maximum(run_max, jnp.max(scores, axis=-1))
    weights_exp = jnp.where(mask_full, jnp.exp(scores - new_max[..., None]), 0.0)
    factor = jnp.exp(run_max - new_max)
    new_total = run_total * factor + jnp.sum(weights_exp, axis=-1)
    new_acc = run_acc * factor[..., None] + jnp.einsum(
        "qhgk,khd->qhgd",
        weights_exp.astype(jnp.bfloat16),
        keyvalue_rows[..., head_dim:],
        preferred_element_type=jnp.float32,
    )
    return (new_max, new_total, new_acc)


def shards(
    prefill_states,
    decode_states,
    attn_gain,
    query_weight,
    keyvalue_weight,
    output_weight,
    cache_keyval,
    cached_length,
    span_tenant,
    ffn_gain,
    expert_in,
    expert_out,
    routes,
    gate_values,
):
    seq_count = lax.axis_size("seq")
    tp_count = lax.axis_size("tp")
    seq_index = lax.axis_index("seq")
    tp_index = lax.axis_index("tp")
    pre_local, model_width = prefill_states.shape
    dec_local = decode_states.shape[0]
    heads_kv = keyvalue_weight.shape[1]
    head_dim = keyvalue_weight.shape[2] // 2
    heads_q = query_weight.shape[1] // head_dim
    query_group_count = heads_q // heads_kv
    score_scale = head_dim ** (-0.5)
    pre_share = pre_local // tp_count
    normalised_input = rms_norm(prefill_states, attn_gain)
    query_matrix = jnp.dot(
        normalised_input, query_weight, preferred_element_type=jnp.float32
    ).reshape(pre_local, heads_q, head_dim)
    keyvalue_rows = jnp.dot(
        normalised_input,
        keyvalue_weight.reshape(model_width, heads_kv * 2 * head_dim),
        preferred_element_type=jnp.float32,
    ).reshape(pre_local, heads_kv, 2 * head_dim)
    before = span_tables(span_tenant)
    token_index = seq_index * pre_local + jnp.arange(pre_local, dtype=jnp.int32)
    tenant, token_positions = token_tables(token_index, span_tenant, before)
    query_matrix = (
        apply_rotary(query_matrix, token_positions)
        .astype(jnp.bfloat16)
        .reshape(pre_local, heads_kv, query_group_count, head_dim)
    )
    rotated_keys = apply_rotary(keyvalue_rows[..., :head_dim], token_positions).astype(jnp.bfloat16)
    local_keyvals = jnp.concatenate(
        [rotated_keys, keyvalue_rows[..., head_dim:].astype(jnp.bfloat16)], axis=-1
    )
    start_state = (
        jnp.full((pre_local, heads_kv, query_group_count), masked_score, jnp.float32),
        jnp.zeros((pre_local, heads_kv, query_group_count), jnp.float32),
        jnp.zeros((pre_local, heads_kv, query_group_count, head_dim), jnp.float32),
    )
    key_piece = lax.all_gather(local_keyvals, "seq", axis=0, tiled=True)
    piece_rows = key_piece.shape[0]
    block_len = math.gcd(piece_rows, key_block)
    blocks = key_piece.reshape(piece_rows // block_len, block_len, heads_kv, 2 * head_dim)

    def one_block(run_state, block_item):
        block_number, block_vals = block_item
        key_index = block_number * block_len + jnp.arange(block_len, dtype=jnp.int32)
        key_tenant = token_tables(key_index, span_tenant, before)[0]
        visible = (tenant[:, None] == key_tenant[None, :]) & (
            token_index[:, None] >= key_index[None, :]
        )
        run_state = attend_keys(run_state, block_vals, visible, query_matrix, score_scale)
        return (run_state, None)

    run_max, run_total, run_acc = lax.scan(
        one_block, start_state, (jnp.arange(piece_rows // block_len, dtype=jnp.int32), blocks)
    )[0]
    attended = (
        (run_acc / run_total[..., None]).astype(jnp.bfloat16).reshape(pre_local, heads_q * head_dim)
    )
    prefill_part = jnp.dot(attended, output_weight, preferred_element_type=jnp.float32)
    all_decode = lax.all_gather(decode_states, ("seq", "tp"), axis=0, tiled=True)
    dec_total = all_decode.shape[0]
    decode_normalised = rms_norm(all_decode, attn_gain)
    decode_queries = jnp.dot(
        decode_normalised, query_weight, preferred_element_type=jnp.float32
    ).reshape(dec_total, heads_q, head_dim)
    decode_queries = (
        apply_rotary(decode_queries, cached_length)
        .astype(jnp.bfloat16)
        .reshape(dec_total, heads_kv, query_group_count, head_dim)
    )
    decode_keyvalues = jnp.dot(
        decode_normalised,
        keyvalue_weight.reshape(model_width, heads_kv * 2 * head_dim),
        preferred_element_type=jnp.float32,
    ).reshape(dec_total, heads_kv, 2 * head_dim)
    new_keys = apply_rotary(decode_keyvalues[..., :head_dim], cached_length).astype(jnp.bfloat16)
    new_vals = decode_keyvalues[..., head_dim:].astype(jnp.bfloat16)
    cache_local = cache_keyval.shape[1]
    cache_pos = seq_index * cache_local + jnp.arange(cache_local, dtype=jnp.int32)
    visible = (cache_pos[None, :] < cached_length[:, None])[:, None, None, :]
    scores = (
        jnp.einsum(
            "bhgd,bkhd->bhgk",
            decode_queries,
            cache_keyval[..., :head_dim],
            preferred_element_type=jnp.float32,
        )
        * score_scale
    )
    scores = jnp.where(visible, scores, masked_score)
    local_max = jnp.max(scores, axis=-1)
    weights_exp = jnp.where(visible, jnp.exp(scores - local_max[..., None]), 0.0)
    local_total = jnp.sum(weights_exp, axis=-1)
    local_acc = jnp.einsum(
        "bhgk,bkhd->bhgd",
        weights_exp.astype(jnp.bfloat16),
        cache_keyval[..., head_dim:],
        preferred_element_type=jnp.float32,
    )
    merged_max = lax.pmax(local_max, "seq")
    shrink = jnp.exp(local_max - merged_max)
    merged_total, merged_acc = (
        lax.psum((local_total * shrink).astype(jnp.bfloat16), "seq").astype(jnp.float32),
        lax.psum((local_acc * shrink[..., None]).astype(jnp.bfloat16), "seq").astype(jnp.float32),
    )
    own_score = (
        jnp.sum(
            decode_queries.astype(jnp.float32) * new_keys.astype(jnp.float32)[:, :, None, :],
            axis=-1,
        )
        * score_scale
    )
    final_max = jnp.maximum(merged_max, own_score)
    rescale = jnp.exp(merged_max - final_max)
    own_exp = jnp.exp(own_score - final_max)
    final_total = merged_total * rescale + own_exp
    own_rounded = lax.optimization_barrier(own_exp.astype(jnp.bfloat16)).astype(jnp.float32)
    final_acc = (
        merged_acc * rescale[..., None]
        + own_rounded[..., None] * new_vals.astype(jnp.float32)[:, :, None, :]
    )
    decode_attended = (
        (final_acc / final_total[..., None])
        .astype(jnp.bfloat16)
        .reshape(dec_total, heads_q * head_dim)
    )
    decode_part = jnp.dot(decode_attended, output_weight, preferred_element_type=jnp.float32)
    group_rows = tp_count * dec_local
    decode_group = lax.dynamic_slice_in_dim(decode_part, seq_index * group_rows, group_rows, 0)
    prefill_full, decode_full = (
        lax.psum(prefill_part.astype(jnp.bfloat16), "tp").astype(jnp.float32),
        lax.psum(decode_group.astype(jnp.bfloat16), "tp").astype(jnp.float32),
    )
    prefill_sum = lax.dynamic_slice_in_dim(prefill_full, tp_index * pre_share, pre_share, 0)
    decode_sum = lax.dynamic_slice_in_dim(decode_full, tp_index * dec_local, dec_local, 0)
    own_states = lax.dynamic_slice_in_dim(prefill_states, tp_index * pre_share, pre_share, 0)
    prefill_h = (own_states.astype(jnp.float32) + prefill_sum).astype(jnp.bfloat16)
    decode_h = (decode_states.astype(jnp.float32) + decode_sum).astype(jnp.bfloat16)
    moe_in = jnp.concatenate([prefill_h, decode_h], axis=0)
    normed_moe = rms_norm(moe_in, ffn_gain)
    rows_dev, top_count = routes.shape
    capacity = 2 * ((rows_dev * top_count + EXPERTS - 1) // EXPERTS)
    flat_routes = routes.reshape(rows_dev * top_count)
    expert_ids = jnp.arange(EXPERTS, dtype=jnp.int32)
    onehot = (flat_routes[:, None] == expert_ids[None, :]).astype(jnp.int32)
    slot_rank = jnp.sum(jnp.cumsum(onehot, axis=0) * onehot, axis=1) - 1
    slot_index = flat_routes * capacity + slot_rank
    repeated = jnp.repeat(normed_moe, top_count, axis=0)
    buffer = jnp.zeros((EXPERTS * capacity, model_width), jnp.bfloat16).at[slot_index].set(repeated)
    outgoing = buffer.reshape(seq_count, EXPERTS // seq_count, capacity, model_width)
    hidden = jnp.einsum(
        "secd,edf->secf",
        lax.all_to_all(outgoing, "seq", split_axis=0, concat_axis=0, tiled=True),
        expert_in,
        preferred_element_type=jnp.float32,
    )
    ff_width = expert_out.shape[1]
    active = (jax.nn.silu(hidden[..., :ff_width]) * hidden[..., ff_width:]).astype(jnp.bfloat16)
    results = jnp.einsum(
        "secf,efd->secd", active, expert_out, preferred_element_type=jnp.float32
    ).astype(jnp.bfloat16)
    returned = lax.all_to_all(results, "seq", split_axis=0, concat_axis=0, tiled=True)
    fetched = (
        returned.reshape(EXPERTS * capacity, model_width)[slot_index]
        .astype(jnp.float32)
        .reshape(rows_dev, top_count, model_width)
    )
    combined = jnp.sum(fetched * gate_values[..., None], axis=1)
    layer_out = (moe_in.astype(jnp.float32) + combined).astype(jnp.bfloat16)
    return (layer_out[:pre_share], layer_out[pre_share:])


def solution(mesh):
    return jax.shard_map(
        shards,
        mesh=mesh,
        in_specs=(
            P("seq", None),
            P(("seq", "tp"), None),
            P(),
            P(None, "tp"),
            P(None, "tp", None),
            P("tp", None),
            P(None, "seq", "tp", None),
            P(),
            P(),
            P(),
            P("seq", None, None),
            P("seq", None, None),
            P(("seq", "tp"), None),
            P(("seq", "tp"), None),
        ),
        out_specs=(P(("seq", "tp"), None), P(("seq", "tp"), None)),
        check_vma=False,
    )
```

profile of v0, /device:TPU:10, one launch (start us, length us, event | category | flops | bytes accessed | tf_op | source)
XLA Modules:
  0.0 792.6 jit_solution(13844461880225228527)
XLA Ops:
  7.3 69.1 %all-gather = bf16[256,1,1536]{2,1,0:T(2,128)(2,1)S(1)} all-gather(bf16[1,1,1536]{2,1,0:T(2,128)(2,1)} %bitcast.217), channel_id=1, replica_groups=mesh['seq'=32,'tp'=8] {'seq','tp'}, dimensions={0}, use_global_device_ids=true | all-gather | bytes 789504 | tf_op jit(solution)/shard_map/all_gather | solution.py:161
  76.4 1.6 convert_element_type.219
  80.8 2.0 fusion.100
  85.4 4.8 fusion.103
  90.2 2.5 fusion.16
  93.4 1.9 copy.118
  95.3 135.8 %pmax.7 = f32[256,1,3]{2,0,1:T(8,128)S(1)} all-reduce(f32[256,1,3]{2,0,1:T(8,128)S(1)} %bitcast.209), channel_id=1, replica_groups=mesh['seq'=32,'tp'=8] {'seq'}, use_global_device_ids=true, to_apply=%region_12.13 | all-reduce | flops 768 | bytes 6144 | tf_op jit(solution)/shard_map/pmax | solution.py:201
  232.8 1.6 fusion.63
  236.0 1.9 convolution_bitcast_fusion.1
  245.4 140.6 %psum.30 = bf16[256,1,3]{2,0,1:T(8,128)(2,1)} all-reduce(bf16[256,1,3]{2,0,1:T(8,128)(2,1)} %get-tuple-element.270), channel_id=1, replica_groups=mesh['seq'=32,'tp'=8] {'seq'}, use_global_device_ids=true, to_apply=%region_16.17 | all-reduce | flops 768 | bytes 3072 | tf_op jit(solution)/shard_map/psum | solution.py:204
  391.8 1.8 fusion.57
  397.0 23.4 %psum.31 = bf16[8,1536]{1,0:T(8,128)(2,1)} all-reduce(bf16[8,1536]{1,0:T(8,128)(2,1)S(1)} %dynamic-slice_convert_fusion), channel_id=1, replica_groups=mesh['seq'=32,'tp'=8] {'tp'}, use_global_device_ids=true, to_apply=%region_17.18 | all-reduce | flops 12288 | bytes 49152 | tf_op jit(solution)/shard_map/psum | solution.py:233
  420.3 31.6 %all-gather.3.cloned.1.call-done = bf16[8192,1,128]{0,2,1:T(8,128)(2,1)} async-done(((bf16[256,1,128]{0,2,1:T(8,128)(2,1)}), bf16[8192,1,128]{0,2,1:T(8,128)(2,1)}) %all-gather.3.cloned.1.call-update) | async-done | bytes 2097168 | tf_op jit(solution)/shard_map/all_gather | solution.py:139
  451.9 3.1 copy.149
  455.1 113.3 %while.17 = (s32[]{:T(128)}, f32[256,1,3]{0,2,1:T(4,128)S(1)}, f32[256,1,3]{0,2,1:T(4,128)S(1)}, f32[256,1,3,64]{0,3,2,1:T(8,128)}, s32[256]{0:T(256)S(1)}, /*in...) while((s32[]{:T(128)}, f32[256,1,3]{0,2,1:T(4,128)S(1)}, ...), condition=%wide.region_8.9_spmd.clone, body=%wide.region_4.8_spmd.clone.sunk | while | flops 104761600 | bytes 14058777 | solution.py:154
  457.6 1.6 fusion.118
  459.1 1.8 fusion.120
  464.6 1.6 fusion.118
  466.2 1.8 fusion.120
  473.3 1.8 fusion.120
  478.8 1.6 fusion.118
  480.4 1.8 fusion.120
  485.9 1.6 fusion.118
  487.5 1.8 fusion.120
  494.6 1.8 fusion.120
  501.6 1.8 fusion.120
  507.1 1.6 fusion.118
  508.7 1.8 fusion.120
  515.8 1.8 fusion.120
  522.9 1.8 fusion.120
  530.0 1.8 fusion.120
  537.0 1.8 fusion.120
  544.1 1.8 fusion.120
  551.2 1.8 fusion.120
  558.3 1.8 fusion.120
  565.4 1.8 fusion.120
  569.4 2.4 convolution_convert_fusion.1
  572.5 63.1 %all-reduce.4.cloned.1.call-done = bf16[256,1536]{1,0:T(8,128)(2,1)} async-done(((bf16[256,1536]{1,0:T(8,128)(2,1)}), bf16[256,1536]{1,0:T(8,128)(2,1)}) %all-reduce.4.cloned.1.call-update) | async-done | bytes 786448 | tf_op jit(solution)/shard_map/psum | solution.py:232
  636.9 3.3 scatter_custom_fusion
  640.1 3.6 reshape.728
  643.7 64.1 %all_to_all.10 = bf16[32,1,18,1536]{3,2,1,0:T(8,128)(2,1)S(1)} all-to-all(bf16[32,1,18,1536]{3,2,1,0:T(8,128)(2,1)} %bitcast.204), channel_id=1, replica_groups=mesh['seq'=32,'tp'=8] {'seq'}, dimensions={0} | all-to-all | bytes 3538944 | tf_op jit(solution)/shard_map/all_to_all | solution.py:254
  707.9 2.0 fusion.23
  711.0 2.4 copy.129
  713.4 6.5 all-to-all-start.1
  720.0 53.1 %all-to-all-done.1 = bf16[32,1,18,1536]{3,2,1,0:T(8,128)(2,1)} async-done(((bf16[32,1,18,1536]{3,2,1,0:T(8,128)(2,1)}), bf16[32,1,18,1536]{3,2,1,0:T(8,128)(2,1)}, u32[]{:S(2)}, u32[]{:S(2)}) %all-to-all-start.1) | async-done | bytes 1769504 | tf_op jit(solution)/shard_map/all_to_all | solution.py:263
  773.2 3.8 reshape.733
  777.0 5.8 gather_fusion
  782.8 2.0 fusion.28
  (401 shorter events, 95.5 us)
Async XLA Ops:
  7.2 700.7 %copy-start = (bf16[1,1536,1024]{2,1,0:T(8,128)(2,1)S(1)}, bf16[1,1536,1024]{2,1,0:T(8,128)(2,1)}, u32[]{:S(2)}) copy-start(bf16[1,1536,1024]{2,1,0:T(8,128)(2,1)} %param.26) | copy-start | bytes 9437188
  7.2 387.4 %all-reduce.6.cloned.1.call-start = ((), (), s32[]{:S(2)}) async-start(), calls=%async_computation.4 | async-start | bytes 196608 | tf_op jit(solution)/shard_map/psum | solution.py:205
  7.2 75.6 %copy-start.27 = (f32[32]{0:T(128)}, f32[32]{0:T(128)S(1)}, u32[]{:S(2)}) copy-start(f32[32]{0:T(128)S(1)} %multiply_power_fusion) | copy-start | bytes 388
  80.8 3.0 copy-start.22
  85.4 4.8 copy-start.30
  234.4 217.5 %all-gather.3.cloned.1.call-start = ((), (), s32[]{:S(2)}) async-start(), calls=%async_computation.2 | async-start | bytes 2162688 | tf_op jit(solution)/shard_map/all_gather | solution.py:139
  234.5 3.5 copy-start.5
  234.5 3.5 copy-start.12
  236.0 2.0 copy-start.29
  236.0 2.6 copy-start.23
  236.0 2.6 copy-start.28
  238.0 5.9 copy-start.8
  238.0 5.9 copy-start.10
  239.6 396.0 %all-reduce.4.cloned.1.call-start = ((), (), s32[]{:S(2)}) async-start(), calls=%async_computation.3 | async-start | bytes 1572864 | tf_op jit(solution)/shard_map/psum | solution.py:232
  240.8 3.0 copy-start.20
  241.8 3.6 copy-start.6
  387.5 6.1 copy-start.13
  387.5 6.1 copy-start.14
  451.9 3.1 copy-start.15
  451.9 3.1 copy-start.19
  459.1 1.9 copy-start.1
  459.1 1.9 copy-start.3
  466.2 1.9 copy-start.1
  466.2 1.9 copy-start.3
  473.3 1.9 copy-start.3
  480.4 1.9 copy-start.1
  480.4 1.9 copy-start.3
  487.5 1.9 copy-start.1
  487.5 1.9 copy-start.3
  494.5 1.9 copy-start.1
  494.5 1.9 copy-start.3
  501.6 1.9 copy-start.3
  508.7 1.9 copy-start.1
  508.7 1.9 copy-start.3
  515.8 1.9 copy-start.1
  515.8 1.9 copy-start.3
  522.9 1.9 copy-start.3
  530.0 1.9 copy-start.3
  537.0 1.9 copy-start.3
  544.1 1.9 copy-start.3
  551.2 1.9 copy-start.3
  558.3 1.9 copy-start.3
  565.4 1.9 copy-start.3
  568.4 3.4 copy-start.17
  568.4 68.4 %copy-start.16 = (f32[1536]{0:T(1024)S(1)}, f32[1536]{0:T(1024)}, u32[]{:S(2)}) copy-start(f32[1536]{0:T(1024)} %convert_element_type.208) | copy-start | bytes 18436
  707.9 2.0 copy-start.31
  713.4 6.5 copy-start.26
  713.4 59.7 %all-to-all-start.1 = ((bf16[32,1,18,1536]{3,2,1,0:T(8,128)(2,1)}), bf16[32,1,18,1536]{3,2,1,0:T(8,128)(2,1)}, u32[]{:S(2)}, u32[]{:S(2)}) async-start(bf16[32,1,18,1536]{3,2,1,0:T(8,128)(2,1)} %copy.129), calls=%async_computation.1 | async-start | bytes 4718592 | tf_op jit(solution)/shard_map/all_to_all | solution.py:263
  (33 other events, 35.6 us)
Sparse Core Ops, SparseCore 0:
  234.6 141.1 all-reduce.5
  378.2 73.6 all-gather.2
  571.9 63.7 all-reduce.3
where the time goes:
time: 800 us; the launch traced here: 793 us
  blocking collectives  433 us (54%)
  waiting for transfers between devices  148 us (18%)
  local copies, waits for them, and re-layouts  67.5 us (8%)
  other arithmetic  59 us (7%)
  matrix products  52.6 us (7%)
  between operations  14.3 us (2%)
  loops' own time  11.6 us (1%)
    psum x1, blocking collectives, shards(): lax.psum((local_total * shrink).astype(jnp.bfloat16), 'seq')  141 us
    pmax x1, blocking collectives, shards(): merged_max = lax.pmax(local_max, 'seq')  136 us
    all_gather x1, blocking collectives, shards(): lax.all_gather(decode_states, ('seq', 'tp'), axis=0, tiled=True)  69.1 us
    all_to_all x1, blocking collectives, shards(): lax.all_to_all(outgoing, 'seq', split_axis=0, concat_axis=0, tiled=True)  64.1 us
    psum x1, waiting for transfers between devices, shards(): lax.psum(prefill_part.astype(jnp.bfloat16), 'tp').astype(jnp.float32)  63.1 us
    all_to_all x1, waiting for transfers between devices, shards(): lax.all_to_all(results, 'seq', split_axis=0, concat_axis=0, tiled=True)  53.1 us
    all_gather x1, waiting for transfers between devices, shards(): key_piece = lax.all_gather(local_keyvals, 'seq', axis=0, tiled=True)  31.6 us
    reduce_sum x16, other arithmetic, attend_keys(): new_total = run_total * factor + jnp.sum(weights_exp, axis=-1)  29.5 us
  transfers between devices with their start and end apart: 4, of which 3 were waited for; matrix products, arithmetic and copies ran while one was open for 3% of the time, Pallas kernels for 0%

commit v1 on v0

--- a/solution.py
+++ b/solution.py
@@ -80,6 +80,62 @@
         preferred_element_type=jnp.float32,
     )
     return (new_max, new_total, new_acc)
+
+
+def swap_partner(values, axis_name, distance):
+    count = lax.axis_size(axis_name)
+    pairs = [(i, i ^ distance) for i in range(count)]
+    return lax.ppermute(values, axis_name, pairs)
+
+
+def gather_blocks(block, axis_name, distances):
+    index = lax.axis_index(axis_name)
+    stacked = block
+    done = []
+    for distance in distances:
+        theirs = swap_partner(stacked, axis_name, distance)
+        upper = (index // distance) % 2 == 1
+        low = jnp.where(upper, theirs, stacked)
+        high = jnp.where(upper, stacked, theirs)
+        place = sum(1 for d in done if d > distance)
+        stacked = jnp.stack([low, high], axis=place)
+        done.append(distance)
+    return stacked.reshape((-1,) + block.shape[1:])
+
+
+def scatter_blocks(values, axis_name, distances, combine, send_type=None):
+    count = lax.axis_size(axis_name)
+    index = lax.axis_index(axis_name)
+    levels = count.bit_length() - 1
+    rows = values.shape[0] // count
+    stacked = values.reshape((2,) * levels + (rows,) + values.shape[1:])
+    remaining = [count >> (j + 1) for j in range(levels)]
+    for distance in distances:
+        place = remaining.index(distance)
+        low = lax.index_in_dim(stacked, 0, place, keepdims=False)
+        high = lax.index_in_dim(stacked, 1, place, keepdims=False)
+        upper = (index // distance) % 2 == 1
+        keep = jnp.where(upper, high, low)
+        send = jnp.where(upper, low, high)
+        if send_type is not None:
+            send = send.astype(send_type)
+        received = swap_partner(send, axis_name, distance).astype(keep.dtype)
+        stacked = combine(keep, received)
+        remaining.pop(place)
+    return stacked
+
+
+def add_parts(first, second):
+    return first + second
+
+
+def merge_softmax(first, second):
+    first_max, second_max = first[..., -1], second[..., -1]
+    top = jnp.maximum(first_max, second_max)
+    first_scale = jnp.exp(first_max - top)[..., None]
+    second_scale = jnp.exp(second_max - top)[..., None]
+    body = first[..., :-1] * first_scale + second[..., :-1] * second_scale
+    return jnp.concatenate([body, top[..., None]], axis=-1)
 
 
 def shards(
@@ -136,7 +192,9 @@
         jnp.zeros((pre_local, heads_kv, query_group_count), jnp.float32),
         jnp.zeros((pre_local, heads_kv, query_group_count, head_dim), jnp.float32),
     )
-    key_piece = lax.all_gather(local_keyvals, "seq", axis=0, tiled=True)
+    seq_near_first = [1 << j for j in range(seq_count.bit_length() - 1)]
+    tp_near_first = [1 << j for j in range(tp_count.bit_length() - 1)]
+    key_piece = gather_blocks(local_keyvals, "seq", seq_near_first[::-1])
     piece_rows = key_piece.shape[0]
     block_len = math.gcd(piece_rows, key_block)
     blocks = key_piece.reshape(piece_rows // block_len, block_len, heads_kv, 2 * head_dim)
@@ -158,24 +216,29 @@
         (run_acc / run_total[..., None]).astype(jnp.bfloat16).reshape(pre_local, heads_q * head_dim)
     )
     prefill_part = jnp.dot(attended, output_weight, preferred_element_type=jnp.float32)
-    all_decode = lax.all_gather(decode_states, ("seq", "tp"), axis=0, tiled=True)
-    dec_total = all_decode.shape[0]
-    decode_normalised = rms_norm(all_decode, attn_gain)
-    decode_queries = jnp.dot(
+    prefill_sum = scatter_blocks(
+        prefill_part, "tp", tp_near_first, add_parts, send_type=jnp.bfloat16
+    )
+    group_states = gather_blocks(decode_states, "tp", tp_near_first[::-1])
+    group_rows = group_states.shape[0]
+    group_lengths = lax.dynamic_slice_in_dim(cached_length, seq_index * group_rows, group_rows, 0)
+    decode_normalised = rms_norm(group_states, attn_gain)
+    group_queries = jnp.dot(
         decode_normalised, query_weight, preferred_element_type=jnp.float32
-    ).reshape(dec_total, heads_q, head_dim)
-    decode_queries = (
-        apply_rotary(decode_queries, cached_length)
+    ).reshape(group_rows, heads_q, head_dim)
+    group_queries = (
+        apply_rotary(group_queries, group_lengths)
         .astype(jnp.bfloat16)
-        .reshape(dec_total, heads_kv, query_group_count, head_dim)
+        .reshape(group_rows, heads_kv, query_group_count, head_dim)
     )
     decode_keyvalues = jnp.dot(
         decode_normalised,
         keyvalue_weight.reshape(model_width, heads_kv * 2 * head_dim),
         preferred_element_type=jnp.float32,
-    ).reshape(dec_total, heads_kv, 2 * head_dim)
-    new_keys = apply_rotary(decode_keyvalues[..., :head_dim], cached_length).astype(jnp.bfloat16)
+    ).reshape(group_rows, heads_kv, 2 * head_dim)
+    new_keys = apply_rotary(decode_keyvalues[..., :head_dim], group_lengths).astype(jnp.bfloat16)
     new_vals = decode_keyvalues[..., head_dim:].astype(jnp.bfloat16)
+    decode_queries = gather_blocks(group_queries, "seq", seq_near_first[::-1])
     cache_local = cache_keyval.shape[1]
     cache_pos = seq_index * cache_local + jnp.arange(cache_local, dtype=jnp.int32)
     visible = (cache_pos[None, :] < cached_length[:, None])[:, None, None, :]
@@ -198,15 +261,14 @@
         cache_keyval[..., head_dim:],
         preferred_element_type=jnp.float32,
     )
-    merged_max = lax.pmax(local_max, "seq")
-    shrink = jnp.exp(local_max - merged_max)
-    merged_total, merged_acc = (
-        lax.psum((local_total * shrink).astype(jnp.bfloat16), "seq").astype(jnp.float32),
-        lax.psum((local_acc * shrink[..., None]).astype(jnp.bfloat16), "seq").astype(jnp.float32),
-    )
+    packed = jnp.concatenate([local_acc, local_total[..., None], local_max[..., None]], axis=-1)
+    merged = scatter_blocks(packed, "seq", seq_near_first, merge_softmax)
+    merged_acc = merged[..., :head_dim]
+    merged_total = merged[..., head_dim]
+    merged_max = merged[..., head_dim + 1]
     own_score = (
         jnp.sum(
-            decode_queries.astype(jnp.float32) * new_keys.astype(jnp.float32)[:, :, None, :],
+            group_queries.astype(jnp.float32) * new_keys.astype(jnp.float32)[:, :, None, :],
             axis=-1,
         )
         * score_scale
@@ -223,17 +285,10 @@
     decode_attended = (
         (final_acc / final_total[..., None])
         .astype(jnp.bfloat16)
-        .reshape(dec_total, heads_q * head_dim)
+        .reshape(group_rows, heads_q * head_dim)
     )
     decode_part = jnp.dot(decode_attended, output_weight, preferred_element_type=jnp.float32)
-    group_rows = tp_count * dec_local
-    decode_group = lax.dynamic_slice_in_dim(decode_part, seq_index * group_rows, group_rows, 0)
-    prefill_full, decode_full = (
-        lax.psum(prefill_part.astype(jnp.bfloat16), "tp").astype(jnp.float32),
-        lax.psum(decode_group.astype(jnp.bfloat16), "tp").astype(jnp.float32),
-    )
-    prefill_sum = lax.dynamic_slice_in_dim(prefill_full, tp_index * pre_share, pre_share, 0)
-    decode_sum = lax.dynamic_slice_in_dim(decode_full, tp_index * dec_local, dec_local, 0)
+    decode_sum = scatter_blocks(decode_part, "tp", tp_near_first, add_parts)
     own_states = lax.dynamic_slice_in_dim(prefill_states, tp_index * pre_share, pre_share, 0)
     prefill_h = (own_states.astype(jnp.float32) + prefill_sum).astype(jnp.bfloat16)
     decode_h = (decode_states.astype(jnp.float32) + decode_sum).astype(jnp.bfloat16)

time: 800 us -> 487 us (0.61)
  the two profiles are of different devices: /device:TPU:10 before, /device:TPU:2 now
where the time goes in v1:
time: 487 us; the launch traced here: 479 us
  waiting for transfers between devices  129 us (26%)
  matrix products  99.5 us (20%)
  local copies, waits for them, and re-layouts  80 us (16%)
  blocking collectives  63.5 us (13%)
  other arithmetic  57.3 us (12%)
  starting transfers between devices  36.4 us (7%)
  loops' own time  11 us (2%)
    ppermute x24, waiting for transfers between devices, swap_partner(): return lax.ppermute(values, axis_name, pairs)  74.9 us
    all_to_all x1, blocking collectives, shards(): lax.all_to_all(outgoing, 'seq', split_axis=0, concat_axis=0, tiled=True)  63.5 us
    all_to_all x1, waiting for transfers between devices, shards(): lax.all_to_all(results, 'seq', split_axis=0, concat_axis=0, tiled=True)  53.8 us
    dot_general x16, matrix products, attend_keys(): jnp.einsum('qhgk,khd->qhgd', weights_exp.astype(jnp.bfloat16), keyvalue_r...  42 us
    dot_general x16, matrix products, attend_keys(): jnp.einsum('qhgd,khd->qhgk', query_matrix, keyvalue_rows[..., :head_dim],...  39.3 us
    dynamic_slice x48, local copies, waits for them, and re-layouts, shards(): lax.scan(one_block, start_state, (jnp.arange(piece_rows // block_len, dty...  35.7 us
    ppermute x24, starting transfers between devices, swap_partner(): return lax.ppermute(values, axis_name, pairs)  29.9 us
    another operation x33, other arithmetic, gather_blocks(): stacked = jnp.stack([low, high], axis=place)  14.3 us
  transfers between devices with their start and end apart: 25, of which 18 were waited for; matrix products, arithmetic and copies ran while one was open for 37% of the time, Pallas kernels for 0%

profile of v1, /device:TPU:2, one launch (start us, length us, event | category | flops | bytes accessed | tf_op | source)
XLA Modules:
  0.0 478.6 jit_solution(8442843845443828296)
XLA Ops:
  7.1 7.2 %collective-permute-start = (bf16[256,1,128]{0,2,1:T(8,128)(2,1)}, bf16[256,1,128]{0,2,1:T(8,128)(2,1)}, u32[]{:S(2)}, u32[]{:S(2)}) collective-permute-start(bf16[256,1,128]{0,2,1:T(8,128)(2,1)} %pad_maximum_fusion.11), channel_id=1, source_target_pairs={{0,128},{8,136},{16,144},{24,152},{32,160},{40,168},{48,176},{56,1... | collective-permute-start | bytes 196616 | tf_op jit(solution)/shard_map/ppermute | solution.py:88
  14.3 3.2 collective-permute-start.8
  35.4 6.0 %collective-permute-done.11 = bf16[8,1,3,64]{3,0,2,1:T(8,128)(2,1)S(1)} collective-permute-done((bf16[8,1,3,64]{3,0,2,1:T(8,128)(2,1)S(1)}, bf16[8,1,3,64]{3,0,2,1:T(8,128)(2,1)S(1)}, u32[]{:S(2)}, u32[]{:S(2)}) %collective-permute-start.11) | collective-permute-done | bytes 3104 | tf_op jit(solution)/shard_map/ppermute | solution.py:88
  43.6 2.5 collective-permute-done.12
  53.2 3.1 collective-permute-done.14
  61.2 4.7 fusion.157
  69.1 3.3 copy.744
  72.3 3.3 copy.745
  78.2 4.7 collective-permute-done.16
  91.7 4.4 collective-permute-done.17
  102.2 3.0 collective-permute-done.18
  110.2 3.2 collective-permute-done.19
  116.5 6.5 %collective-permute-done.20 = f32[8,1,3,66]{3,0,2,1:T(8,128)S(1)} collective-permute-done((f32[8,1,3,66]{3,0,2,1:T(8,128)S(1)}, f32[8,1,3,66]{3,0,2,1:T(8,128)S(1)}, u32[]{:S(2)}, u32[]{:S(2)}) %collective-permute-start.20) | collective-permute-done | bytes 6368 | tf_op jit(solution)/shard_map/ppermute | solution.py:88
  130.6 12.2 %collective-permute-done.3 = bf16[2,2,2,256,1,128]{3,5,0,1,2,4:T(8,128)(2,1)} collective-permute-done((bf16[2,2,2,256,1,128]{3,5,0,1,2,4:T(8,128)(2,1)}, bf16[2,2,2,256,1,128]{3,5,0,1,2,4:T(8,128)(2,1)}, u32[]{:S(2)}, u32[]{:S(2)}) %collective-permute-start.3) | collective-permute-done | bytes 524320 | tf_op jit(solution)/shard_map/ppermute | solution.py:88
  149.5 12.1 %collective-permute-done.4 = bf16[2,2,2,2,256,1,128]{4,6,0,1,2,3,5:T(8,128)(2,1)} collective-permute-done((bf16[2,2,2,2,256,1,128]{4,6,0,1,2,3,5:T(8,128)(2,1)}, bf16[2,2,2,2,256,1,128]{4,6,0,1,2,3,5:T(8,128)(2,1)}, u32[]{:S(2)}, u32[]{:S(2)}) %collective-permute-start.4) | collective-permute-done | bytes 1048608 | tf_op jit(solution)/shard_map/ppermute | solution.py:88
  166.2 4.2 copy.706
  170.9 138.5 %while.17 = (s32[]{:T(128)}, f32[256,1,3]{0,2,1:T(4,128)S(1)}, f32[256,1,3]{0,2,1:T(4,128)S(1)}, f32[256,1,3,64]{0,3,2,1:T(8,128)}, s32[256]{0:T(256)S(1)}, /*in...) while((s32[]{:T(128)}, f32[256,1,3]{0,2,1:T(4,128)S(1)}, ...), condition=%wide.region_8.9_spmd.clone, body=%wide.region_4.8_spmd.clone.sunk | while | flops 104761600 | bytes 12748093 | solution.py:212
  176.5 2.6 fusion.184
  185.2 2.6 fusion.184
  191.4 2.5 fusion.181
  193.9 2.6 fusion.184
  200.0 2.5 fusion.181
  202.5 2.6 fusion.184
  208.7 2.5 fusion.181
  211.2 2.6 fusion.184
  217.3 2.5 fusion.181
  219.8 2.6 fusion.184
  226.0 2.5 fusion.181
  228.5 2.6 fusion.184
  234.7 2.5 fusion.181
  237.1 2.6 fusion.184
  245.8 2.6 fusion.184
  254.5 2.6 fusion.184
  263.1 2.6 fusion.184
  271.8 2.6 fusion.184
  280.4 2.6 fusion.184
  289.1 2.6 fusion.184
  297.7 2.6 fusion.184
  306.4 2.6 fusion.184
  316.9 4.4 collective-permute-done.6
  323.0 4.6 collective-permute-done.7
  328.8 3.3 scatter_custom_fusion
  332.1 3.6 reshape.1399
  335.7 63.5 %all_to_all.10 = bf16[32,1,18,1536]{3,2,1,0:T(8,128)(2,1)S(1)} all-to-all(bf16[32,1,18,1536]{3,2,1,0:T(8,128)(2,1)} %bitcast.449), channel_id=1, replica_groups=mesh['seq'=32,'tp'=8] {'seq'}, dimensions={0} | all-to-all | bytes 3538944 | tf_op jit(solution)/shard_map/all_to_all | solution.py:309
  404.8 6.5 %all-to-all-start.1 = ((bf16[32,1,18,1536]{3,2,1,0:T(8,128)(2,1)}), bf16[32,1,18,1536]{3,2,1,0:T(8,128)(2,1)}, u32[]{:S(2)}, u32[]{:S(2)}) async-start(bf16[32,1,18,1536]{3,2,1,0:T(8,128)(2,1)} %copy.790), calls=%async_computation.1 | async-start | bytes 4718592 | tf_op jit(solution)/shard_map/all_to_all | solution.py:318
  411.4 53.8 %all-to-all-done.1 = bf16[32,1,18,1536]{3,2,1,0:T(8,128)(2,1)} async-done(((bf16[32,1,18,1536]{3,2,1,0:T(8,128)(2,1)}), bf16[32,1,18,1536]{3,2,1,0:T(8,128)(2,1)}, u32[]{:S(2)}, u32[]{:S(2)}) %all-to-all-start.1) | async-done | bytes 1769504 | tf_op jit(solution)/shard_map/all_to_all | solution.py:318
  465.2 3.8 reshape.1404
  469.0 5.8 %gather_fusion = bf16[264,1536]{1,0:T(8,128)(2,1)} fusion(bf16[576,1536]{1,0:T(8,128)(2,1)} %reshape.1404, s32[1024]{0:T(1024)S(1)} %pad_clamp_fusion), kind=kCustom, calls=%fused_computation | custom fusion | bytes 1623072 | tf_op jit(solution)/shard_map/gather | solution.py:320
  (539 shorter events, 175.9 us)
Async XLA Ops:
  0.6 398.6 %copy-start = (bf16[1,1536,1024]{2,1,0:T(8,128)(2,1)S(1)}, bf16[1,1536,1024]{2,1,0:T(8,128)(2,1)}, u32[]{:S(2)}) copy-start(bf16[1,1536,1024]{2,1,0:T(8,128)(2,1)} %param.26) | copy-start | bytes 9437188
  0.6 17.7 %copy-start.32 = (s32[33,8]{0,1:T(8,128)S(1)}, s32[33,8]{0,1:T(8,128)}, u32[]{:S(2)}) copy-start(s32[33,8]{0,1:T(8,128)} %param.28) | copy-start | bytes 3172
  0.7 20.2 %copy-start.35 = (f32[32]{0:T(128)}, f32[32]{0:T(128)S(1)}, u32[]{:S(2)}) copy-start(f32[32]{0:T(128)S(1)} %multiply_power_fusion) | copy-start | bytes 388
  6.3 14.6 %copy-start.42 = (s32[256]{0:T(256)S(1)}, s32[256]{0:T(256)}, u32[]{:S(2)}) copy-start(s32[256]{0:T(256)} %param.23) | copy-start | bytes 3076
  7.1 45.1 %collective-permute-start = (bf16[256,1,128]{0,2,1:T(8,128)(2,1)}, bf16[256,1,128]{0,2,1:T(8,128)(2,1)}, u32[]{:S(2)}, u32[]{:S(2)}) collective-permute-start(bf16[256,1,128]{0,2,1:T(8,128)(2,1)} %pad_maximum_fusion.11), channel_id=1, source_target_pairs={{0,128},{8,136},{16,144},{24,152},{32,160},{40,168},{48,176},{56,1... | collective-permute-start | bytes 196616 | tf_op jit(solution)/shard_map/ppermute | solution.py:88
  14.3 9.7 %collective-permute-start.8 = (bf16[1,1536]{1,0:T(2,128)(2,1)}, bf16[1,1536]{1,0:T(2,128)(2,1)}, u32[]{:S(2)}, u32[]{:S(2)}) collective-permute-start(bf16[1,1536]{1,0:T(2,128)(2,1)} %param.17), channel_id=1, source_target_pairs={{0,4},{1,5},{2,6},{3,7},{4,0},{5,1},{6,2},{7,3},{8,12},{9,13},{10,... | collective-permute-start | bytes 9224 | tf_op jit(solution)/shard_map/ppermute | solution.py:88
  23.9 9.6 %copy-start.33 = (f32[8,32]{1,0:T(8,128)S(1)}, f32[8,32]{1,0:T(8,128)}, u32[]{:S(2)}) copy-start(f32[8,32]{1,0:T(8,128)} %get-tuple-element.311) | copy-start | bytes 3076
  23.9 9.6 %copy-start.34 = (f32[8,32]{1,0:T(8,128)S(1)}, f32[8,32]{1,0:T(8,128)}, u32[]{:S(2)}) copy-start(f32[8,32]{1,0:T(8,128)} %get-tuple-element.312) | copy-start | bytes 3076
  24.8 3.7 collective-permute-start.9
  28.5 1.3 collective-permute-start.10
  33.8 32.1 %copy-start.28 = (f32[8,3]{0,1:T(4,128)}, f32[8,3]{0,1:T(4,128)S(1)}, u32[]{:S(2)}) copy-start(f32[8,3]{0,1:T(4,128)S(1)} %get-tuple-element.266) | copy-start | bytes 292
  33.8 7.6 %collective-permute-start.11 = (bf16[8,1,3,64]{3,0,2,1:T(8,128)(2,1)S(1)}, bf16[8,1,3,64]{3,0,2,1:T(8,128)(2,1)S(1)}, u32[]{:S(2)}, u32[]{:S(2)}) collective-permute-start(bf16[8,1,3,64]{3,0,2,1:T(8,128)(2,1)S(1)} %get-tuple-element.267), channel_id=1, source_target_pairs={{0,128},{8,136},{16,144},{24,152},{32,160},{40,168},{48,176},{56,1... | collective-permute-start | bytes 9224 | tf_op jit(solution)/shard_map/ppermute | solution.py:88
  41.4 4.7 collective-permute-start.12
  46.1 3.9 collective-permute-start.13
  50.1 6.2 %collective-permute-start.14 = (bf16[2,2,2,8,1,3,64]{6,3,5,0,1,2,4:T(8,128)(2,1)S(1)}, bf16[2,2,2,8,1,3,64]{6,3,5,0,1,2,4:T(8,128)(2,1)S(1)}, u32[]{:S(2)}, u32[]{:S(2)}) collective-permute-start(bf16[2,2,2,8,1,3,64]{6,3,5,0,1,2,4:T(8,128)(2,1)S(1)} %fusion.101), channel_id=1, source_target_pairs={{0,16},{8,24},{16,0},{24,8},{32,48},{40,56},{48,32},{56,40},{64,80... | collective-permute-start | bytes 73736 | tf_op jit(solution)/shard_map/ppermute | solution.py:88
  56.3 4.7 collective-permute-start.15
  57.1 20.1 %collective-permute-start.1 = (bf16[2,256,1,128]{1,3,0,2:T(8,128)(2,1)}, bf16[2,256,1,128]{1,3,0,2:T(8,128)(2,1)}, u32[]{:S(2)}, u32[]{:S(2)}) collective-permute-start(bf16[2,256,1,128]{1,3,0,2:T(8,128)(2,1)} %fusion.82), channel_id=1, source_target_pairs={{0,64},{8,72},{16,80},{24,88},{32,96},{40,104},{48,112},{56,120},{... | collective-permute-start | bytes 393224 | tf_op jit(solution)/shard_map/ppermute | solution.py:88
  61.2 4.7 copy-start.43
  77.1 5.8 %copy-start.9 = (f32[2,2,2,2,8,1,3,66]{7,4,6,0,1,2,5,3:T(8,128)}, f32[2,2,2,2,8,1,3,66]{7,4,6,0,1,2,5,3:T(8,128)S(1)}, u32[]{:S(2)}) copy-start(f32[2,2,2,2,8,1,3,66]{7,4,6,0,1,2,5,3:T(8,128)S(1)} %get-tuple-element.290) | copy-start | bytes 304132
  77.1 5.8 %collective-permute-start.16 = (f32[2,2,2,2,8,1,3,66]{7,4,6,5,3,2,1,0:T(8,128)S(1)}, f32[2,2,2,2,8,1,3,66]{7,4,6,5,3,2,1,0:T(8,128)S(1)}, u32[]{:S(2)}, u32[]{:S(2)}) collective-permute-start(f32[2,2,2,2,8,1,3,66]{7,4,6,5,3,2,1,0:T(8,128)S(1)} %copy.746), channel_id=1, source_target_pairs={{0,8},{8,0},{16,24},{24,16},{32,40},{40,32},{48,56},{56,48},{64,72... | collective-permute-start | bytes 304136 | tf_op jit(solution)/shard_map/ppermute | solution.py:88
  89.8 6.2 %collective-permute-start.17 = (f32[2,2,2,8,1,3,66]{6,3,5,4,2,1,0:T(8,128)S(1)}, f32[2,2,2,8,1,3,66]{6,3,5,4,2,1,0:T(8,128)S(1)}, u32[]{:S(2)}, u32[]{:S(2)}) collective-permute-start(f32[2,2,2,8,1,3,66]{6,3,5,4,2,1,0:T(8,128)S(1)} %copy.753), channel_id=1, source_target_pairs={{0,16},{8,24},{16,0},{24,8},{32,48},{40,56},{48,32},{56,40},{64,80... | collective-permute-start | bytes 152072 | tf_op jit(solution)/shard_map/ppermute | solution.py:88
  91.6 18.5 %copy-start.13 = (bf16[1,256,1,128]{1,3,2,0:T(8,128)(2,1)S(1)}, bf16[1,256,1,128]{1,3,2,0:T(8,128)(2,1)}, u32[]{:S(2)}) copy-start(bf16[1,256,1,128]{1,3,2,0:T(8,128)(2,1)} %copy-done.11) | copy-start | bytes 196612
  91.6 18.5 %copy-start.16 = (bf16[1,256,1,128]{1,3,2,0:T(8,128)(2,1)S(1)}, bf16[1,256,1,128]{1,3,2,0:T(8,128)(2,1)}, u32[]{:S(2)}) copy-start(bf16[1,256,1,128]{1,3,2,0:T(8,128)(2,1)} %copy-done.14) | copy-start | bytes 196612
  100.9 22.4 %copy-start.26 = (f32[8,1,3,1]{3,0,2,1:T(8,128)S(1)}, f32[8,1,3,1]{3,0,2,1:T(8,128)}, u32[]{:S(2)}) copy-start(f32[8,1,3,1]{3,0,2,1:T(8,128)} %copy.772) | copy-start | bytes 292
  101.0 4.2 collective-permute-start.18
  108.6 4.8 %copy-start.24 = (f32[2,8,1,3,66]{4,1,3,2,0:T(8,128)}, f32[2,8,1,3,66]{4,1,3,2,0:T(8,128)S(1)}, u32[]{:S(2)}) copy-start(f32[2,8,1,3,66]{4,1,3,2,0:T(8,128)S(1)} %get-tuple-element.273) | copy-start | bytes 38020
  108.7 4.8 collective-permute-start.19
  110.2 13.9 %copy-start.8 = (bf16[2,1,256,1,128]{2,4,0,3,1:T(8,128)(2,1)}, bf16[2,1,256,1,128]{2,4,0,3,1:T(8,128)(2,1)S(1)}, u32[]{:S(2)}) copy-start(bf16[2,1,256,1,128]{2,4,0,3,1:T(8,128)(2,1)S(1)} %select_bitcast_fusion.5) | copy-start | bytes 393220
  115.3 13.8 %copy-start.31 = (f32[8,64]{1,0:T(8,128)S(1)}, f32[8,64]{1,0:T(8,128)}, u32[]{:S(2)}) copy-start(f32[8,64]{1,0:T(8,128)} %bitcast_convert_fusion) | copy-start | bytes 6148
  115.4 7.6 %collective-permute-start.20 = (f32[8,1,3,66]{3,0,2,1:T(8,128)S(1)}, f32[8,1,3,66]{3,0,2,1:T(8,128)S(1)}, u32[]{:S(2)}, u32[]{:S(2)}) collective-permute-start(f32[8,1,3,66]{3,0,2,1:T(8,128)S(1)} %select_bitcast_fusion.17), channel_id=1, source_target_pairs={{0,128},{8,136},{16,144},{24,152},{32,160},{40,168},{48,176},{56,1... | collective-permute-start | bytes 19016 | tf_op jit(solution)/shard_map/ppermute | solution.py:88
  115.4 8.7 %collective-permute-start.2 = (bf16[2,2,256,1,128]{2,4,0,1,3:T(8,128)(2,1)S(1)}, bf16[2,2,256,1,128]{2,4,0,1,3:T(8,128)(2,1)S(1)}, u32[]{:S(2)}, u32[]{:S(2)}) collective-permute-start(bf16[2,2,256,1,128]{2,4,0,1,3:T(8,128)(2,1)S(1)} %fusion.76), channel_id=1, source_target_pairs={{0,32},{8,40},{16,48},{24,56},{32,0},{40,8},{48,16},{56,24},{64,96... | collective-permute-start | bytes 786440 | tf_op jit(solution)/shard_map/ppermute | solution.py:88
  127.6 15.3 %collective-permute-start.3 = (bf16[2,2,2,256,1,128]{3,5,0,1,2,4:T(8,128)(2,1)}, bf16[2,2,2,256,1,128]{3,5,0,1,2,4:T(8,128)(2,1)}, u32[]{:S(2)}, u32[]{:S(2)}) collective-permute-start(bf16[2,2,2,256,1,128]{3,5,0,1,2,4:T(8,128)(2,1)} %fusion.58), channel_id=1, source_target_pairs={{0,16},{8,24},{16,0},{24,8},{32,48},{40,56},{48,32},{56,40},{64,80... | collective-permute-start | bytes 1572872 | tf_op jit(solution)/shard_map/ppermute | solution.py:88
  129.3 14.5 %copy-start.7 = (bf16[2,2,1,256,1,128]{3,5,0,1,4,2:T(8,128)(2,1)S(1)}, bf16[2,2,1,256,1,128]{3,5,0,1,4,2:T(8,128)(2,1)}, u32[]{:S(2)}) copy-start(bf16[2,2,1,256,1,128]{3,5,0,1,4,2:T(8,128)(2,1)} %copy-done.6) | copy-start | bytes 786436
  146.4 15.3 %collective-permute-start.4 = (bf16[2,2,2,2,256,1,128]{4,6,0,1,2,3,5:T(8,128)(2,1)}, bf16[2,2,2,2,256,1,128]{4,6,0,1,2,3,5:T(8,128)(2,1)}, u32[]{:S(2)}, u32[]{:S(2)}) collective-permute-start(bf16[2,2,2,2,256,1,128]{4,6,0,1,2,3,5:T(8,128)(2,1)} %fusion.42), channel_id=1, source_target_pairs={{0,8},{8,0},{16,24},{24,16},{32,40},{40,32},{48,56},{56,48},{64,72... | collective-permute-start | bytes 3145736 | tf_op jit(solution)/shard_map/ppermute | solution.py:88
  146.8 1.3 collective-permute-start.21
  148.2 15.1 %copy-start.22 = (f32[2,2,1,1536]{3,2,1,0:T(1,128)}, f32[2,2,1,1536]{3,2,1,0:T(1,128)S(1)}, u32[]{:S(2)}) copy-start(f32[2,2,1,1536]{3,2,1,0:T(1,128)S(1)} %fusion.103) | copy-start | bytes 73732
  148.9 14.5 %copy-start.3 = (bf16[2,2,2,1,256,1,128]{4,6,0,1,2,5,3:T(8,128)(2,1)S(1)}, bf16[2,2,2,1,256,1,128]{4,6,0,1,2,5,3:T(8,128)(2,1)}, u32[]{:S(2)}) copy-start(bf16[2,2,2,1,256,1,128]{4,6,0,1,2,5,3:T(8,128)(2,1)} %copy-done.2) | copy-start | bytes 1572868
  148.9 14.5 %copy-start.5 = (bf16[2,2,2,1,256,1,128]{4,6,0,1,2,5,3:T(8,128)(2,1)S(1)}, bf16[2,2,2,1,256,1,128]{4,6,0,1,2,5,3:T(8,128)(2,1)}, u32[]{:S(2)}) copy-start(bf16[2,2,2,1,256,1,128]{4,6,0,1,2,5,3:T(8,128)(2,1)} %copy-done.4) | copy-start | bytes 1572868
  148.9 163.5 %collective-permute-start.22 = (f32[2,1,1536]{2,1,0:T(1,128)}, f32[2,1,1536]{2,1,0:T(1,128)}, u32[]{:S(2)}, u32[]{:S(2)}) collective-permute-start(f32[2,1,1536]{2,1,0:T(1,128)} %fusion.118), channel_id=1, source_target_pairs={{0,2},{1,3},{2,0},{3,1},{4,6},{5,7},{6,4},{7,5},{8,10},{9,11},{10,... | collective-permute-start | bytes 36872 | tf_op jit(solution)/shard_map/ppermute | solution.py:88
  166.2 4.7 copy-start.29
  312.2 1.8 collective-permute-start.5
  314.2 14.6 %copy-start.27 = (f32[1536]{0:T(1024)S(1)}, f32[1536]{0:T(1024)}, u32[]{:S(2)}) copy-start(f32[1536]{0:T(1024)} %convert_element_type.259) | copy-start | bytes 18436
  314.2 14.7 %copy-start.36 = (s32[264]{0:T(512)S(1)}, s32[264]{0:T(512)}, u32[]{:S(2)}) copy-start(s32[264]{0:T(512)} %fusion.150) | copy-start | bytes 3172
  314.2 7.1 %collective-permute-start.6 = (bf16[2,32,1536]{2,1,0:T(8,128)(2,1)S(1)}, bf16[2,32,1536]{2,1,0:T(8,128)(2,1)S(1)}, u32[]{:S(2)}, u32[]{:S(2)}) collective-permute-start(bf16[2,32,1536]{2,1,0:T(8,128)(2,1)S(1)} %fusion.72), channel_id=1, source_target_pairs={{0,2},{1,3},{2,0},{3,1},{4,6},{5,7},{6,4},{7,5},{8,10},{9,11},{10,... | collective-permute-start | bytes 589832 | tf_op jit(solution)/shard_map/ppermute | solution.py:88
  315.0 7.3 %collective-permute-start.23 = (f32[1,1536]{1,0:T(1,128)S(1)}, f32[1,1536]{1,0:T(1,128)S(1)}, u32[]{:S(2)}, u32[]{:S(2)}) collective-permute-start(f32[1,1536]{1,0:T(1,128)S(1)} %fusion.128), channel_id=1, source_target_pairs={{0,4},{1,5},{2,6},{3,7},{4,0},{5,1},{6,2},{7,3},{8,12},{9,13},{10,... | collective-permute-start | bytes 18440 | tf_op jit(solution)/shard_map/ppermute | solution.py:88
  321.4 6.2 %collective-permute-start.7 = (bf16[32,1536]{1,0:T(8,128)(2,1)S(1)}, bf16[32,1536]{1,0:T(8,128)(2,1)S(1)}, u32[]{:S(2)}, u32[]{:S(2)}) collective-permute-start(bf16[32,1536]{1,0:T(8,128)(2,1)S(1)} %fusion.79), channel_id=1, source_target_pairs={{0,4},{1,5},{2,6},{3,7},{4,0},{5,1},{6,2},{7,3},{8,12},{9,13},{10,... | collective-permute-start | bytes 294920 | tf_op jit(solution)/shard_map/ppermute | solution.py:88
  404.8 6.5 %copy-start.40 = (f32[33,8]{0,1:T(8,128)S(1)}, f32[33,8]{0,1:T(8,128)}, u32[]{:S(2)}) copy-start(f32[33,8]{0,1:T(8,128)} %param.29) | copy-start | bytes 3172
  404.8 60.4 %all-to-all-start.1 = ((bf16[32,1,18,1536]{3,2,1,0:T(8,128)(2,1)}), bf16[32,1,18,1536]{3,2,1,0:T(8,128)(2,1)}, u32[]{:S(2)}, u32[]{:S(2)}) async-start(bf16[32,1,18,1536]{3,2,1,0:T(8,128)(2,1)} %copy.790), calls=%async_computation.1 | async-start | bytes 4718592 | tf_op jit(solution)/shard_map/all_to_all | solution.py:318
  (52 other events, 131.5 us)

commit v2 on v1

--- a/solution.py
+++ b/solution.py
@@ -123,6 +123,36 @@
         stacked = combine(keep, received)
         remaining.pop(place)
     return stacked
+
+
+def exchange_all(chunks, axis_name):
+    count = lax.axis_size(axis_name)
+    index = lax.axis_index(axis_name)
+    pieces = [lax.dynamic_index_in_dim(chunks, index, 0, keepdims=False)]
+    for shift in range(1, count):
+        outgoing = lax.dynamic_index_in_dim(chunks, (index - shift) % count, 0, keepdims=False)
+        pairs = [(i, (i - shift) % count) for i in range(count)]
+        pieces.append(lax.ppermute(outgoing, axis_name, pairs))
+    return jnp.roll(jnp.stack(pieces), index, axis=0)
+
+
+def gather_direct(block, axis_name):
+    count = lax.axis_size(axis_name)
+    index = lax.axis_index(axis_name)
+    pieces = [block]
+    for shift in range(1, count):
+        pairs = [(i, (i - shift) % count) for i in range(count)]
+        pieces.append(lax.ppermute(block, axis_name, pairs))
+    gathered = jnp.roll(jnp.stack(pieces), index, axis=0)
+    return gathered.reshape((-1,) + block.shape[1:])
+
+
+def scatter_direct(values, axis_name, send_type=None):
+    count = lax.axis_size(axis_name)
+    chunks = values.reshape((count, values.shape[0] // count) + values.shape[1:])
+    if send_type is not None:
+        chunks = chunks.astype(send_type)
+    return exchange_all(chunks, axis_name).astype(values.dtype)
 
 
 def add_parts(first, second):
@@ -187,39 +217,72 @@
     local_keyvals = jnp.concatenate(
         [rotated_keys, keyvalue_rows[..., head_dim:].astype(jnp.bfloat16)], axis=-1
     )
-    start_state = (
-        jnp.full((pre_local, heads_kv, query_group_count), masked_score, jnp.float32),
-        jnp.zeros((pre_local, heads_kv, query_group_count), jnp.float32),
-        jnp.zeros((pre_local, heads_kv, query_group_count, head_dim), jnp.float32),
-    )
     seq_near_first = [1 << j for j in range(seq_count.bit_length() - 1)]
-    tp_near_first = [1 << j for j in range(tp_count.bit_length() - 1)]
     key_piece = gather_blocks(local_keyvals, "seq", seq_near_first[::-1])
     piece_rows = key_piece.shape[0]
     block_len = math.gcd(piece_rows, key_block)
     blocks = key_piece.reshape(piece_rows // block_len, block_len, heads_kv, 2 * head_dim)
+    query_count = pre_local * query_group_count
+    query_rows = query_matrix.transpose(1, 0, 2, 3).reshape(heads_kv, query_count, head_dim)
+    row_token = jnp.repeat(token_index, query_group_count)
+    row_tenant = jnp.repeat(tenant, query_group_count)
+    start_state = (
+        jnp.full((heads_kv, query_count), masked_score, jnp.float32),
+        jnp.zeros((heads_kv, query_count), jnp.float32),
+        jnp.zeros((heads_kv, query_count, head_dim), jnp.float32),
+    )
 
     def one_block(run_state, block_item):
         block_number, block_vals = block_item
         key_index = block_number * block_len + jnp.arange(block_len, dtype=jnp.int32)
         key_tenant = token_tables(key_index, span_tenant, before)[0]
-        visible = (tenant[:, None] == key_tenant[None, :]) & (
+        token_visible = (tenant[:, None] == key_tenant[None, :]) & (
             token_index[:, None] >= key_index[None, :]
         )
-        run_state = attend_keys(run_state, block_vals, visible, query_matrix, score_scale)
+
+        def attend(state):
+            run_max, run_total, run_acc = state
+            visible = (row_tenant[:, None] == key_tenant[None, :]) & (
+                row_token[:, None] >= key_index[None, :]
+            )
+            scores = (
+                jnp.einsum(
+                    "hqd,khd->hqk",
+                    query_rows,
+                    block_vals[..., :head_dim],
+                    preferred_element_type=jnp.float32,
+                )
+                * score_scale
+            )
+            scores = jnp.where(visible[None], scores, masked_score)
+            new_max = jnp.maximum(run_max, jnp.max(scores, axis=-1))
+            weights_exp = jnp.where(visible[None], jnp.exp(scores - new_max[..., None]), 0.0)
+            factor = jnp.exp(run_max - new_max)
+            new_total = run_total * factor + jnp.sum(weights_exp, axis=-1)
+            new_acc = run_acc * factor[..., None] + jnp.einsum(
+                "hqk,khd->hqd",
+                weights_exp.astype(jnp.bfloat16),
+                block_vals[..., head_dim:],
+                preferred_element_type=jnp.float32,
+            )
+            return (new_max, new_total, new_acc)
+
+        run_state = lax.cond(jnp.any(token_visible), attend, lambda state: state, run_state)
         return (run_state, None)
 
     run_max, run_total, run_acc = lax.scan(
         one_block, start_state, (jnp.arange(piece_rows // block_len, dtype=jnp.int32), blocks)
     )[0]
     attended = (
-        (run_acc / run_total[..., None]).astype(jnp.bfloat16).reshape(pre_local, heads_q * head_dim)
+        (run_acc / run_total[..., None])
+        .astype(jnp.bfloat16)
+        .reshape(heads_kv, pre_local, query_group_count, head_dim)
+        .transpose(1, 0, 2, 3)
+        .reshape(pre_local, heads_q * head_dim)
     )
     prefill_part = jnp.dot(attended, output_weight, preferred_element_type=jnp.float32)
-    prefill_sum = scatter_blocks(
-        prefill_part, "tp", tp_near_first, add_parts, send_type=jnp.bfloat16
-    )
-    group_states = gather_blocks(decode_states, "tp", tp_near_first[::-1])
+    prefill_sum = jnp.sum(scatter_direct(prefill_part, "tp", send_type=jnp.bfloat16), axis=0)
+    group_states = gather_direct(decode_states, "tp")
     group_rows = group_states.shape[0]
     group_lengths = lax.dynamic_slice_in_dim(cached_length, seq_index * group_rows, group_rows, 0)
     decode_normalised = rms_norm(group_states, attn_gain)
@@ -238,7 +301,7 @@
     ).reshape(group_rows, heads_kv, 2 * head_dim)
     new_keys = apply_rotary(decode_keyvalues[..., :head_dim], group_lengths).astype(jnp.bfloat16)
     new_vals = decode_keyvalues[..., head_dim:].astype(jnp.bfloat16)
-    decode_queries = gather_blocks(group_queries, "seq", seq_near_first[::-1])
+    decode_queries = gather_direct(group_queries, "seq")
     cache_local = cache_keyval.shape[1]
     cache_pos = seq_index * cache_local + jnp.arange(cache_local, dtype=jnp.int32)
     visible = (cache_pos[None, :] < cached_length[:, None])[:, None, None, :]
@@ -262,10 +325,13 @@
         preferred_element_type=jnp.float32,
     )
     packed = jnp.concatenate([local_acc, local_total[..., None], local_max[..., None]], axis=-1)
-    merged = scatter_blocks(packed, "seq", seq_near_first, merge_softmax)
+    parts = scatter_direct(packed, "seq")
+    part_max = parts[..., -1]
+    merged_max = jnp.max(part_max, axis=0)
+    part_scale = jnp.exp(part_max - merged_max[None])
+    merged = jnp.sum(parts[..., :-1] * part_scale[..., None], axis=0)
     merged_acc = merged[..., :head_dim]
     merged_total = merged[..., head_dim]
-    merged_max = merged[..., head_dim + 1]
     own_score = (
         jnp.sum(
             group_queries.astype(jnp.float32) * new_keys.astype(jnp.float32)[:, :, None, :],
@@ -288,7 +354,7 @@
         .reshape(group_rows, heads_q * head_dim)
     )
     decode_part = jnp.dot(decode_attended, output_weight, preferred_element_type=jnp.float32)
-    decode_sum = scatter_blocks(decode_part, "tp", tp_near_first, add_parts)
+    decode_sum = jnp.sum(scatter_direct(decode_part, "tp"), axis=0)
     own_states = lax.dynamic_slice_in_dim(prefill_states, tp_index * pre_share, pre_share, 0)
     prefill_h = (own_states.astype(jnp.float32) + prefill_sum).astype(jnp.bfloat16)
     decode_h = (decode_states.astype(jnp.float32) + decode_sum).astype(jnp.bfloat16)
@@ -306,7 +372,7 @@
     outgoing = buffer.reshape(seq_count, EXPERTS // seq_count, capacity, model_width)
     hidden = jnp.einsum(
         "secd,edf->secf",
-        lax.all_to_all(outgoing, "seq", split_axis=0, concat_axis=0, tiled=True),
+        exchange_all(outgoing, "seq"),
         expert_in,
         preferred_element_type=jnp.float32,
     )
@@ -315,7 +381,7 @@
     results = jnp.einsum(
         "secf,efd->secd", active, expert_out, preferred_element_type=jnp.float32
     ).astype(jnp.bfloat16)
-    returned = lax.all_to_all(results, "seq", split_axis=0, concat_axis=0, tiled=True)
+    returned = exchange_all(results, "seq")
     fetched = (
         returned.reshape(EXPERTS * capacity, model_width)[slot_index]
         .astype(jnp.float32)

time: 487 us -> 928 us (1.91)
  the two profiles are of different devices: /device:TPU:2 before, /device:TPU:10 now
where the time goes in v2:
time: 928 us; the launch traced here: 911 us
  starting transfers between devices  504 us (54%)
  local copies, waits for them, and re-layouts  213 us (23%)
  waiting for transfers between devices  96.1 us (10%)
  other arithmetic  48.4 us (5%)
  matrix products  23.3 us (3%)
  loops' own time  22.9 us (2%)
    ppermute x107, starting transfers between devices, exchange_all(): pieces.append(lax.ppermute(outgoing, axis_name, pairs))  346 us
    ppermute x38, starting transfers between devices, gather_direct(): pieces.append(lax.ppermute(block, axis_name, pairs))  111 us
    dynamic_slice x33, local copies, waits for them, and re-layouts, exchange_all(): lax.dynamic_index_in_dim(chunks, (index - shift) % count, 0, keepdims=False)  75.6 us
    ppermute x5, waiting for transfers between devices, swap_partner(): return lax.ppermute(values, axis_name, pairs)  55.9 us
    ppermute x5, starting transfers between devices, swap_partner(): return lax.ppermute(values, axis_name, pairs)  46.9 us
    another operation x33, local copies, waits for them, and re-layouts, exchange_all(): return jnp.roll(jnp.stack(pieces), index, axis=0)  44.5 us
    concatenate x3, local copies, waits for them, and re-layouts, exchange_all(): return jnp.roll(jnp.stack(pieces), index, axis=0)  38.6 us
    ppermute x107, waiting for transfers between devices, exchange_all(): pieces.append(lax.ppermute(outgoing, axis_name, pairs))  35.9 us
  transfers between devices with their start and end apart: 150, of which 27 were waited for; matrix products, arithmetic and copies ran while one was open for 20% of the time, Pallas kernels for 0%

profile of v2, /device:TPU:10, one launch (start us, length us, event | category | flops | bytes accessed | tf_op | source)
XLA Modules:
  0.0 910.6 jit_solution(8453107209424972812)
XLA Ops:
  0.7 12.7 %collective-permute-start.12 = (bf16[1,1536]{1,0:T(2,128)(2,1)}, bf16[1,1536]{1,0:T(2,128)(2,1)}, u32[]{:S(2)}, u32[]{:S(2)}) collective-permute-start(bf16[1,1536]{1,0:T(2,128)(2,1)} %param.21), channel_id=1, source_target_pairs={{0,7},{1,0},{2,1},{3,2},{4,3},{5,4},{6,5},{7,6},{8,15},{9,8},{10,9... | collective-permute-start | bytes 9224 | tf_op jit(solution)/shard_map/ppermute | solution.py:145
  13.4 11.8 %collective-permute-start.13 = (bf16[1,1536]{1,0:T(2,128)(2,1)}, bf16[1,1536]{1,0:T(2,128)(2,1)}, u32[]{:S(2)}, u32[]{:S(2)}) collective-permute-start(bf16[1,1536]{1,0:T(2,128)(2,1)} %param.21), channel_id=1, source_target_pairs={{0,6},{1,7},{2,0},{3,1},{4,2},{5,3},{6,4},{7,5},{8,14},{9,15},{10,... | collective-permute-start | bytes 9224 | tf_op jit(solution)/shard_map/ppermute | solution.py:145
  62.1 5.9 collective-permute-start.20
  84.4 5.5 collective-permute-start.29
  96.2 4.5 collective-permute-start.33
  100.7 4.6 collective-permute-start.34
  112.7 4.7 collective-permute-start.38
  121.8 4.4 collective-permute-start.41
  144.8 4.7 fusion.123
  156.5 7.2 constant_dynamic-slice_fusion.27
  165.1 4.6 collective-permute-start.50
  181.1 6.5 collective-permute-start.55
  206.4 16.5 %constant_dynamic-slice_fusion.9 = (f32[1,8,1,3,66]{0,1,4,3,2:T(8,128)}, f32[1,8,1,3,66]{0,1,4,3,2:T(8,128)}, f32[1,8,1,3,66]{0,1,4,3,2:T(8,128)}, f32[1,8,1,3,6...) fusion(f32[32,8,1,3,66]{0,1,4,3,2:T(8,128)} %copy-done.1, ...), kind=kLoop, calls=%fused_computation.424 | loop fusion | bytes 228168 | tf_op jit(solution)/shard_map/jit(dynamic_index_in_dim)/dynamic_slice | solution.py:133
  238.4 5.9 collective-permute-start.64
  257.9 6.0 collective-permute-start.68
  282.2 5.4 collective-permute-start.72
  360.2 38.6 %concatenate.134 = f32[64,8,1,3,66]{0,1,4,3,2:T(8,128)} concatenate(f32[1,8,1,3,66]{0,1,4,3,2:T(8,128)} %get-tuple-element.837, f32[1,8,1,3,66]{0,1,4,3,2:T(8,128)} %copy.4018, f32[1,8,1,3,66]{0,1,4,3,2:T(8,128)} %copy.4019, f32[1,8,1,3,66]{0,1,4,3,2:T(8,128)} %copy.4020, f32[1,8,1,3,66]{0,1,4,3,2:T(8,128)} %copy.4021, f32[1,8,1,3,66]{0,1,4,3,2:T(8,128)} %copy.4022, ...), dimensions={0} | concatenate | bytes 811008 | tf_op jit(solution)/shard_map/jit(_roll_dynamic)/concatenate | solution.py:136
  403.9 8.2 collective-permute-start.81
  412.1 11.9 %collective-permute-start.82 = (f32[1,1536]{1,0:T(1,128)S(1)}, f32[1,1536]{1,0:T(1,128)S(1)}, u32[]{:S(2)}, u32[]{:S(2)}) collective-permute-start(f32[1,1536]{1,0:T(1,128)S(1)} %get-tuple-element.861), channel_id=1, source_target_pairs={{0,6},{1,7},{2,0},{3,1},{4,2},{5,3},{6,4},{7,5},{8,14},{9,15},{10,... | collective-permute-start | bytes 18440 | tf_op jit(solution)/shard_map/ppermute | solution.py:135
  433.3 11.6 %collective-permute-start.1 = (bf16[2,256,1,128]{1,3,2,0:T(8,128)(2,1)S(1)}, bf16[2,256,1,128]{1,3,2,0:T(8,128)(2,1)S(1)}, u32[]{:S(2)}, u32[]{:S(2)}) collective-permute-start(bf16[2,256,1,128]{1,3,2,0:T(8,128)(2,1)S(1)} %pad_maximum_fusion.6), channel_id=1, source_target_pairs={{0,64},{8,72},{16,80},{24,88},{32,96},{40,104},{48,112},{56,120},{... | collective-permute-start | bytes 393224 | tf_op jit(solution)/shard_map/ppermute | solution.py:88
  444.9 9.4 %collective-permute-done.1 = bf16[2,256,1,128]{1,3,2,0:T(8,128)(2,1)S(1)} collective-permute-done((bf16[2,256,1,128]{1,3,2,0:T(8,128)(2,1)S(1)}, bf16[2,256,1,128]{1,3,2,0:T(8,128)(2,1)S(1)}, u32[]{:S(2)}, u32[]{:S(2)}) %collective-permute-start.1) | collective-permute-done | bytes 131104 | tf_op jit(solution)/shard_map/ppermute | solution.py:88
  454.4 10.2 %collective-permute-start.2 = (bf16[2,2,256,1,128]{2,4,0,3,1:T(8,128)(2,1)S(1)}, bf16[2,2,256,1,128]{2,4,0,3,1:T(8,128)(2,1)S(1)}, u32[]{:S(2)}, u32[]{:S(2)}) collective-permute-start(bf16[2,2,256,1,128]{2,4,0,3,1:T(8,128)(2,1)S(1)} %pad_maximum_fusion.4), channel_id=1, source_target_pairs={{0,32},{8,40},{16,48},{24,56},{32,0},{40,8},{48,16},{56,24},{64,96... | collective-permute-start | bytes 786440 | tf_op jit(solution)/shard_map/ppermute | solution.py:88
  464.6 8.3 collective-permute-done.2
  473.0 11.1 %collective-permute-start.3 = (bf16[2,2,2,256,1,128]{3,5,0,1,4,2:T(8,128)(2,1)S(1)}, bf16[2,2,2,256,1,128]{3,5,0,1,4,2:T(8,128)(2,1)S(1)}, u32[]{:S(2)}, u32[]{:S(2)}) collective-permute-start(bf16[2,2,2,256,1,128]{3,5,0,1,4,2:T(8,128)(2,1)S(1)} %pad_maximum_fusion.3), channel_id=1, source_target_pairs={{0,16},{8,24},{16,0},{24,8},{32,48},{40,56},{48,32},{56,40},{64,80... | collective-permute-start | bytes 1572872 | tf_op jit(solution)/shard_map/ppermute | solution.py:88
  484.1 14.3 %collective-permute-done.3 = bf16[2,2,2,256,1,128]{3,5,0,1,4,2:T(8,128)(2,1)S(1)} collective-permute-done((bf16[2,2,2,256,1,128]{3,5,0,1,4,2:T(8,128)(2,1)S(1)}, bf16[2,2,2,256,1,128]{3,5,0,1,4,2:T(8,128)(2,1)S(1)}, u32[]{:S(2)}, u32[]{:S(2)}) %collective-permute-start.3) | collective-permute-done | bytes 524320 | tf_op jit(solution)/shard_map/ppermute | solution.py:88
  498.5 11.2 %collective-permute-start.4 = (bf16[2,2,2,2,256,1,128]{4,6,0,1,2,5,3:T(8,128)(2,1)S(1)}, bf16[2,2,2,2,256,1,128]{4,6,0,1,2,5,3:T(8,128)(2,1)S(1)}, u32[]{:S(2)}, u32[]{:S(2)}) collective-permute-start(bf16[2,2,2,2,256,1,128]{4,6,0,1,2,5,3:T(8,128)(2,1)S(1)} %pad_maximum_fusion.1), channel_id=1, source_target_pairs={{0,8},{8,0},{16,24},{24,16},{32,40},{40,32},{48,56},{56,48},{64,72... | collective-permute-start | bytes 3145736 | tf_op jit(solution)/shard_map/ppermute | solution.py:88
  509.8 23.9 %collective-permute-done.4 = bf16[2,2,2,2,256,1,128]{4,6,0,1,2,5,3:T(8,128)(2,1)S(1)} collective-permute-done((bf16[2,2,2,2,256,1,128]{4,6,0,1,2,5,3:T(8,128)(2,1)S(1)}, bf16[2,2,2,2,256,1,128]{4,6,0,1,2,5,3:T(8,128)(2,1)S(1)}, u32[]{:S(2)}, u32[]{:S(2)}) %collective-permute-start.4) | collective-permute-done | bytes 1048608 | tf_op jit(solution)/shard_map/ppermute | solution.py:88
  540.3 55.8 %while.18 = (s32[]{:T(128)}, f32[1,768]{1,0:T(1,128)S(1)}, f32[1,768]{1,0:T(1,128)S(1)}, f32[1,768,64]{1,2,0:T(8,128)}, s32[256]{0:T(256)S(1)}, /*index=5*/s32[1...) while((s32[]{:T(128)}, f32[1,768]{1,0:T(1,128)S(1)}, ...), condition=%wide.region_11.12_spmd.clone.clone, body=%wide.region_4.11_spmd.clone.clone.sunk | while | flops 108380672 | bytes 5859667 | solution.py:273
  543.4 5.7 conditional.4
  598.9 51.4 %collective-permute-start.5 = (bf16[32,1536]{1,0:T(8,128)(2,1)S(1)}, bf16[32,1536]{1,0:T(8,128)(2,1)S(1)}, u32[]{:S(2)}, u32[]{:S(2)}) collective-permute-start(bf16[32,1536]{1,0:T(8,128)(2,1)S(1)} %get-tuple-element.845), channel_id=1, source_target_pairs={{0,7},{1,0},{2,1},{3,2},{4,3},{5,4},{6,5},{7,6},{8,15},{9,8},{10,9... | collective-permute-start | bytes 294920 | tf_op jit(solution)/shard_map/ppermute | solution.py:135
  650.4 11.9 %collective-permute-start.6 = (bf16[32,1536]{1,0:T(8,128)(2,1)S(1)}, bf16[32,1536]{1,0:T(8,128)(2,1)S(1)}, u32[]{:S(2)}, u32[]{:S(2)}) collective-permute-start(bf16[32,1536]{1,0:T(8,128)(2,1)S(1)} %get-tuple-element.844), channel_id=1, source_target_pairs={{0,6},{1,7},{2,0},{3,1},{4,2},{5,3},{6,4},{7,5},{8,14},{9,15},{10,... | collective-permute-start | bytes 294920 | tf_op jit(solution)/shard_map/ppermute | solution.py:135
  687.5 6.4 collective-permute-start.89
  701.7 4.4 collective-permute-start.95
  710.4 5.5 collective-permute-start.98
  724.1 4.6 collective-permute-start.102
  737.5 4.4 collective-permute-start.105
  747.8 4.4 collective-permute-start.108
  752.3 7.7 collective-permute-start.109
  763.2 6.6 collective-permute-start.113
  782.7 4.5 collective-permute-done.117
  805.9 4.9 collective-permute-start.124
  827.3 6.0 collective-permute-start.132
  833.3 4.9 collective-permute-start.133
  842.0 4.8 collective-permute-start.135
  849.4 6.0 collective-permute-start.137
  858.3 5.3 collective-permute-start.140
  867.2 5.8 collective-permute-start.142
  901.3 5.8 gather_fusion
  (804 shorter events, 460.3 us)
Async XLA Ops:
  0.7 50.1 %collective-permute-start.12 = (bf16[1,1536]{1,0:T(2,128)(2,1)}, bf16[1,1536]{1,0:T(2,128)(2,1)}, u32[]{:S(2)}, u32[]{:S(2)}) collective-permute-start(bf16[1,1536]{1,0:T(2,128)(2,1)} %param.21), channel_id=1, source_target_pairs={{0,7},{1,0},{2,1},{3,2},{4,3},{5,4},{6,5},{7,6},{8,15},{9,8},{10,9... | collective-permute-start | bytes 9224 | tf_op jit(solution)/shard_map/ppermute | solution.py:145
  13.4 38.0 %collective-permute-start.13 = (bf16[1,1536]{1,0:T(2,128)(2,1)}, bf16[1,1536]{1,0:T(2,128)(2,1)}, u32[]{:S(2)}, u32[]{:S(2)}) collective-permute-start(bf16[1,1536]{1,0:T(2,128)(2,1)} %param.21), channel_id=1, source_target_pairs={{0,6},{1,7},{2,0},{3,1},{4,2},{5,3},{6,4},{7,5},{8,14},{9,15},{10,... | collective-permute-start | bytes 9224 | tf_op jit(solution)/shard_map/ppermute | solution.py:145
  25.2 26.9 %collective-permute-start.14 = (bf16[1,1536]{1,0:T(2,128)(2,1)}, bf16[1,1536]{1,0:T(2,128)(2,1)}, u32[]{:S(2)}, u32[]{:S(2)}) collective-permute-start(bf16[1,1536]{1,0:T(2,128)(2,1)} %param.21), channel_id=1, source_target_pairs={{0,5},{1,6},{2,7},{3,0},{4,1},{5,2},{6,3},{7,4},{8,13},{9,14},{10,... | collective-permute-start | bytes 9224 | tf_op jit(solution)/shard_map/ppermute | solution.py:145
  27.1 25.0 %collective-permute-start.15 = (bf16[1,1536]{1,0:T(2,128)(2,1)}, bf16[1,1536]{1,0:T(2,128)(2,1)}, u32[]{:S(2)}, u32[]{:S(2)}) collective-permute-start(bf16[1,1536]{1,0:T(2,128)(2,1)} %param.21), channel_id=1, source_target_pairs={{0,4},{1,5},{2,6},{3,7},{4,0},{5,1},{6,2},{7,3},{8,12},{9,13},{10,... | collective-permute-start | bytes 9224 | tf_op jit(solution)/shard_map/ppermute | solution.py:145
  28.5 23.7 %collective-permute-start.16 = (bf16[1,1536]{1,0:T(2,128)(2,1)}, bf16[1,1536]{1,0:T(2,128)(2,1)}, u32[]{:S(2)}, u32[]{:S(2)}) collective-permute-start(bf16[1,1536]{1,0:T(2,128)(2,1)} %param.21), channel_id=1, source_target_pairs={{0,3},{1,4},{2,5},{3,6},{4,7},{5,0},{6,1},{7,2},{8,11},{9,12},{10,... | collective-permute-start | bytes 9224 | tf_op jit(solution)/shard_map/ppermute | solution.py:145
  171.2 23.9 %collective-permute-start.51 = (f32[8,1,3,66]{3,0,2,1:T(8,128)S(1)}, f32[8,1,3,66]{3,0,2,1:T(8,128)S(1)}, u32[]{:S(2)}, u32[]{:S(2)}) collective-permute-start(f32[8,1,3,66]{3,0,2,1:T(8,128)S(1)} %bitcast.1010), channel_id=1, source_target_pairs={{0,240},{8,248},{16,0},{24,8},{32,16},{40,24},{48,32},{56,40},{64,... | collective-permute-start | bytes 19016 | tf_op jit(solution)/shard_map/ppermute | solution.py:135
  172.9 22.3 %collective-permute-start.52 = (f32[8,1,3,66]{3,0,2,1:T(8,128)S(1)}, f32[8,1,3,66]{3,0,2,1:T(8,128)S(1)}, u32[]{:S(2)}, u32[]{:S(2)}) collective-permute-start(f32[8,1,3,66]{3,0,2,1:T(8,128)S(1)} %bitcast.1009), channel_id=1, source_target_pairs={{0,232},{8,240},{16,248},{24,0},{32,8},{40,16},{48,24},{56,32},{64... | collective-permute-start | bytes 19016 | tf_op jit(solution)/shard_map/ppermute | solution.py:135
  175.6 21.7 %collective-permute-start.53 = (f32[8,1,3,66]{3,0,2,1:T(8,128)S(1)}, f32[8,1,3,66]{3,0,2,1:T(8,128)S(1)}, u32[]{:S(2)}, u32[]{:S(2)}) collective-permute-start(f32[8,1,3,66]{3,0,2,1:T(8,128)S(1)} %bitcast.1008), channel_id=1, source_target_pairs={{0,224},{8,232},{16,240},{24,248},{32,0},{40,8},{48,16},{56,24},{6... | collective-permute-start | bytes 19016 | tf_op jit(solution)/shard_map/ppermute | solution.py:135
  178.1 21.3 %collective-permute-start.54 = (f32[8,1,3,66]{3,0,2,1:T(8,128)S(1)}, f32[8,1,3,66]{3,0,2,1:T(8,128)S(1)}, u32[]{:S(2)}, u32[]{:S(2)}) collective-permute-start(f32[8,1,3,66]{3,0,2,1:T(8,128)S(1)} %bitcast.1006), channel_id=1, source_target_pairs={{0,216},{8,224},{16,232},{24,240},{32,248},{40,0},{48,8},{56,16},{... | collective-permute-start | bytes 19016 | tf_op jit(solution)/shard_map/ppermute | solution.py:135
  181.1 21.7 %collective-permute-start.55 = (f32[8,1,3,66]{3,0,2,1:T(8,128)S(1)}, f32[8,1,3,66]{3,0,2,1:T(8,128)S(1)}, u32[]{:S(2)}, u32[]{:S(2)}) collective-permute-start(f32[8,1,3,66]{3,0,2,1:T(8,128)S(1)} %bitcast.1005), channel_id=1, source_target_pairs={{0,208},{8,216},{16,224},{24,232},{32,240},{40,248},{48,0},{56,8},... | collective-permute-start | bytes 19016 | tf_op jit(solution)/shard_map/ppermute | solution.py:135
  195.1 35.3 %collective-permute-start.56 = (f32[8,1,3,66]{3,0,2,1:T(8,128)S(1)}, f32[8,1,3,66]{3,0,2,1:T(8,128)S(1)}, u32[]{:S(2)}, u32[]{:S(2)}) collective-permute-start(f32[8,1,3,66]{3,0,2,1:T(8,128)S(1)} %bitcast.1028), channel_id=1, source_target_pairs={{0,200},{8,208},{16,216},{24,224},{32,232},{40,240},{48,248},{56,0... | collective-permute-start | bytes 19016 | tf_op jit(solution)/shard_map/ppermute | solution.py:135
  195.2 36.4 %collective-permute-start.57 = (f32[8,1,3,66]{3,0,2,1:T(8,128)S(1)}, f32[8,1,3,66]{3,0,2,1:T(8,128)S(1)}, u32[]{:S(2)}, u32[]{:S(2)}) collective-permute-start(f32[8,1,3,66]{3,0,2,1:T(8,128)S(1)} %bitcast.1026), channel_id=1, source_target_pairs={{0,192},{8,200},{16,208},{24,216},{32,224},{40,232},{48,240},{56,2... | collective-permute-start | bytes 19016 | tf_op jit(solution)/shard_map/ppermute | solution.py:135
  197.4 37.0 %collective-permute-start.58 = (f32[8,1,3,66]{3,0,2,1:T(8,128)S(1)}, f32[8,1,3,66]{3,0,2,1:T(8,128)S(1)}, u32[]{:S(2)}, u32[]{:S(2)}) collective-permute-start(f32[8,1,3,66]{3,0,2,1:T(8,128)S(1)} %bitcast.1024), channel_id=1, source_target_pairs={{0,184},{8,192},{16,200},{24,208},{32,216},{40,224},{48,232},{56,2... | collective-permute-start | bytes 19016 | tf_op jit(solution)/shard_map/ppermute | solution.py:135
  199.4 39.0 %collective-permute-start.59 = (f32[8,1,3,66]{3,0,2,1:T(8,128)S(1)}, f32[8,1,3,66]{3,0,2,1:T(8,128)S(1)}, u32[]{:S(2)}, u32[]{:S(2)}) collective-permute-start(f32[8,1,3,66]{3,0,2,1:T(8,128)S(1)} %bitcast.1022), channel_id=1, source_target_pairs={{0,176},{8,184},{16,192},{24,200},{32,208},{40,216},{48,224},{56,2... | collective-permute-start | bytes 19016 | tf_op jit(solution)/shard_map/ppermute | solution.py:135
  202.8 41.6 %collective-permute-start.60 = (f32[8,1,3,66]{3,0,2,1:T(8,128)S(1)}, f32[8,1,3,66]{3,0,2,1:T(8,128)S(1)}, u32[]{:S(2)}, u32[]{:S(2)}) collective-permute-start(f32[8,1,3,66]{3,0,2,1:T(8,128)S(1)} %bitcast.1021), channel_id=1, source_target_pairs={{0,168},{8,176},{16,184},{24,192},{32,200},{40,208},{48,216},{56,2... | collective-permute-start | bytes 19016 | tf_op jit(solution)/shard_map/ppermute | solution.py:135
  230.3 23.4 %collective-permute-start.61 = (f32[8,1,3,66]{3,0,2,1:T(8,128)S(1)}, f32[8,1,3,66]{3,0,2,1:T(8,128)S(1)}, u32[]{:S(2)}, u32[]{:S(2)}) collective-permute-start(f32[8,1,3,66]{3,0,2,1:T(8,128)S(1)} %bitcast.1030), channel_id=1, source_target_pairs={{0,160},{8,168},{16,176},{24,184},{32,192},{40,200},{48,208},{56,2... | collective-permute-start | bytes 19016 | tf_op jit(solution)/shard_map/ppermute | solution.py:135
  231.6 25.9 %collective-permute-start.62 = (f32[8,1,3,66]{3,0,2,1:T(8,128)S(1)}, f32[8,1,3,66]{3,0,2,1:T(8,128)S(1)}, u32[]{:S(2)}, u32[]{:S(2)}) collective-permute-start(f32[8,1,3,66]{3,0,2,1:T(8,128)S(1)} %bitcast.1029), channel_id=1, source_target_pairs={{0,152},{8,160},{16,168},{24,176},{32,184},{40,192},{48,200},{56,2... | collective-permute-start | bytes 19016 | tf_op jit(solution)/shard_map/ppermute | solution.py:135
  234.3 23.5 %collective-permute-start.63 = (f32[8,1,3,66]{3,0,2,1:T(8,128)S(1)}, f32[8,1,3,66]{3,0,2,1:T(8,128)S(1)}, u32[]{:S(2)}, u32[]{:S(2)}) collective-permute-start(f32[8,1,3,66]{3,0,2,1:T(8,128)S(1)} %bitcast.1027), channel_id=1, source_target_pairs={{0,144},{8,152},{16,160},{24,168},{32,176},{40,184},{48,192},{56,2... | collective-permute-start | bytes 19016 | tf_op jit(solution)/shard_map/ppermute | solution.py:135
  238.4 25.5 %collective-permute-start.64 = (f32[8,1,3,66]{3,0,2,1:T(8,128)S(1)}, f32[8,1,3,66]{3,0,2,1:T(8,128)S(1)}, u32[]{:S(2)}, u32[]{:S(2)}) collective-permute-start(f32[8,1,3,66]{3,0,2,1:T(8,128)S(1)} %bitcast.1025), channel_id=1, source_target_pairs={{0,136},{8,144},{16,152},{24,160},{32,168},{40,176},{48,184},{56,1... | collective-permute-start | bytes 19016 | tf_op jit(solution)/shard_map/ppermute | solution.py:135
  244.3 23.5 %collective-permute-start.65 = (f32[8,1,3,66]{3,0,2,1:T(8,128)S(1)}, f32[8,1,3,66]{3,0,2,1:T(8,128)S(1)}, u32[]{:S(2)}, u32[]{:S(2)}) collective-permute-start(f32[8,1,3,66]{3,0,2,1:T(8,128)S(1)} %bitcast.1023), channel_id=1, source_target_pairs={{0,128},{8,136},{16,144},{24,152},{32,160},{40,168},{48,176},{56,1... | collective-permute-start | bytes 19016 | tf_op jit(solution)/shard_map/ppermute | solution.py:135
  253.7 24.5 %collective-permute-start.66 = (f32[8,1,3,66]{3,0,2,1:T(8,128)S(1)}, f32[8,1,3,66]{3,0,2,1:T(8,128)S(1)}, u32[]{:S(2)}, u32[]{:S(2)}) collective-permute-start(f32[8,1,3,66]{3,0,2,1:T(8,128)S(1)} %bitcast.1014), channel_id=1, source_target_pairs={{0,120},{8,128},{16,136},{24,144},{32,152},{40,160},{48,168},{56,1... | collective-permute-start | bytes 19016 | tf_op jit(solution)/shard_map/ppermute | solution.py:135
  257.5 24.7 %collective-permute-start.67 = (f32[8,1,3,66]{3,0,2,1:T(8,128)S(1)}, f32[8,1,3,66]{3,0,2,1:T(8,128)S(1)}, u32[]{:S(2)}, u32[]{:S(2)}) collective-permute-start(f32[8,1,3,66]{3,0,2,1:T(8,128)S(1)} %bitcast.1013), channel_id=1, source_target_pairs={{0,112},{8,120},{16,128},{24,136},{32,144},{40,152},{48,160},{56,1... | collective-permute-start | bytes 19016 | tf_op jit(solution)/shard_map/ppermute | solution.py:135
  257.9 29.8 %collective-permute-start.68 = (f32[8,1,3,66]{3,0,2,1:T(8,128)S(1)}, f32[8,1,3,66]{3,0,2,1:T(8,128)S(1)}, u32[]{:S(2)}, u32[]{:S(2)}) collective-permute-start(f32[8,1,3,66]{3,0,2,1:T(8,128)S(1)} %bitcast.1012), channel_id=1, source_target_pairs={{0,104},{8,112},{16,120},{24,128},{32,136},{40,144},{48,152},{56,1... | collective-permute-start | bytes 19016 | tf_op jit(solution)/shard_map/ppermute | solution.py:135
  263.9 23.7 %collective-permute-start.69 = (f32[8,1,3,66]{3,0,2,1:T(8,128)S(1)}, f32[8,1,3,66]{3,0,2,1:T(8,128)S(1)}, u32[]{:S(2)}, u32[]{:S(2)}) collective-permute-start(f32[8,1,3,66]{3,0,2,1:T(8,128)S(1)} %bitcast.1011), channel_id=1, source_target_pairs={{0,96},{8,104},{16,112},{24,120},{32,128},{40,136},{48,144},{56,15... | collective-permute-start | bytes 19016 | tf_op jit(solution)/shard_map/ppermute | solution.py:135
  267.8 20.8 %collective-permute-start.70 = (f32[8,1,3,66]{3,0,2,1:T(8,128)S(1)}, f32[8,1,3,66]{3,0,2,1:T(8,128)S(1)}, u32[]{:S(2)}, u32[]{:S(2)}) collective-permute-start(f32[8,1,3,66]{3,0,2,1:T(8,128)S(1)} %bitcast.1007), channel_id=1, source_target_pairs={{0,88},{8,96},{16,104},{24,112},{32,120},{40,128},{48,136},{56,144... | collective-permute-start | bytes 19016 | tf_op jit(solution)/shard_map/ppermute | solution.py:135
  278.2 23.6 %collective-permute-start.71 = (f32[8,1,3,66]{3,0,2,1:T(8,128)}, f32[8,1,3,66]{3,0,2,1:T(8,128)S(1)}, u32[]{:S(2)}, u32[]{:S(2)}) collective-permute-start(f32[8,1,3,66]{3,0,2,1:T(8,128)} %bitcast.131), channel_id=1, source_target_pairs={{0,80},{8,88},{16,96},{24,104},{32,112},{40,120},{48,128},{56,136}... | collective-permute-start | bytes 19016 | tf_op jit(solution)/shard_map/ppermute | solution.py:135
  282.2 23.8 %collective-permute-start.72 = (f32[8,1,3,66]{3,0,2,1:T(8,128)}, f32[8,1,3,66]{3,0,2,1:T(8,128)S(1)}, u32[]{:S(2)}, u32[]{:S(2)}) collective-permute-start(f32[8,1,3,66]{3,0,2,1:T(8,128)} %bitcast.133), channel_id=1, source_target_pairs={{0,72},{8,80},{16,88},{24,96},{32,104},{40,112},{48,120},{56,128},... | collective-permute-start | bytes 19016 | tf_op jit(solution)/shard_map/ppermute | solution.py:135
  287.6 20.6 %collective-permute-start.73 = (f32[8,1,3,66]{3,0,2,1:T(8,128)}, f32[8,1,3,66]{3,0,2,1:T(8,128)S(1)}, u32[]{:S(2)}, u32[]{:S(2)}) collective-permute-start(f32[8,1,3,66]{3,0,2,1:T(8,128)} %bitcast.135), channel_id=1, source_target_pairs={{0,64},{8,72},{16,80},{24,88},{32,96},{40,104},{48,112},{56,120},{... | collective-permute-start | bytes 19016 | tf_op jit(solution)/shard_map/ppermute | solution.py:135
  287.7 20.6 %collective-permute-start.74 = (f32[8,1,3,66]{3,0,2,1:T(8,128)}, f32[8,1,3,66]{3,0,2,1:T(8,128)S(1)}, u32[]{:S(2)}, u32[]{:S(2)}) collective-permute-start(f32[8,1,3,66]{3,0,2,1:T(8,128)} %bitcast.137), channel_id=1, source_target_pairs={{0,56},{8,64},{16,72},{24,80},{32,88},{40,96},{48,104},{56,112},{6... | collective-permute-start | bytes 19016 | tf_op jit(solution)/shard_map/ppermute | solution.py:135
  288.6 22.0 %collective-permute-start.75 = (f32[8,1,3,66]{3,0,2,1:T(8,128)}, f32[8,1,3,66]{3,0,2,1:T(8,128)}, u32[]{:S(2)}, u32[]{:S(2)}) collective-permute-start(f32[8,1,3,66]{3,0,2,1:T(8,128)} %bitcast.139), channel_id=1, source_target_pairs={{0,48},{8,56},{16,64},{24,72},{32,80},{40,88},{48,96},{56,104},{64... | collective-permute-start | bytes 19016 | tf_op jit(solution)/shard_map/ppermute | solution.py:135
  301.8 45.5 %collective-permute-start.76 = (f32[8,1,3,66]{3,0,2,1:T(8,128)}, f32[8,1,3,66]{3,0,2,1:T(8,128)}, u32[]{:S(2)}, u32[]{:S(2)}) collective-permute-start(f32[8,1,3,66]{3,0,2,1:T(8,128)} %bitcast.1020), channel_id=1, source_target_pairs={{0,40},{8,48},{16,56},{24,64},{32,72},{40,80},{48,88},{56,96},{64,... | collective-permute-start | bytes 19016 | tf_op jit(solution)/shard_map/ppermute | solution.py:135
  306.0 46.1 %collective-permute-start.77 = (f32[8,1,3,66]{3,0,2,1:T(8,128)}, f32[8,1,3,66]{3,0,2,1:T(8,128)}, u32[]{:S(2)}, u32[]{:S(2)}) collective-permute-start(f32[8,1,3,66]{3,0,2,1:T(8,128)} %bitcast.1019), channel_id=1, source_target_pairs={{0,32},{8,40},{16,48},{24,56},{32,64},{40,72},{48,80},{56,88},{64,... | collective-permute-start | bytes 19016 | tf_op jit(solution)/shard_map/ppermute | solution.py:135
  308.2 46.0 %collective-permute-start.78 = (f32[8,1,3,66]{3,0,2,1:T(8,128)}, f32[8,1,3,66]{3,0,2,1:T(8,128)}, u32[]{:S(2)}, u32[]{:S(2)}) collective-permute-start(f32[8,1,3,66]{3,0,2,1:T(8,128)} %bitcast.1018), channel_id=1, source_target_pairs={{0,24},{8,32},{16,40},{24,48},{32,56},{40,64},{48,72},{56,80},{64,... | collective-permute-start | bytes 19016 | tf_op jit(solution)/shard_map/ppermute | solution.py:135
  308.2 48.0 %collective-permute-start.79 = (f32[8,1,3,66]{3,0,2,1:T(8,128)}, f32[8,1,3,66]{3,0,2,1:T(8,128)}, u32[]{:S(2)}, u32[]{:S(2)}) collective-permute-start(f32[8,1,3,66]{3,0,2,1:T(8,128)} %bitcast.1017), channel_id=1, source_target_pairs={{0,16},{8,24},{16,32},{24,40},{32,48},{40,56},{48,64},{56,72},{64,... | collective-permute-start | bytes 19016 | tf_op jit(solution)/shard_map/ppermute | solution.py:135
  310.6 47.6 %collective-permute-start.80 = (f32[8,1,3,66]{3,0,2,1:T(8,128)}, f32[8,1,3,66]{3,0,2,1:T(8,128)}, u32[]{:S(2)}, u32[]{:S(2)}) collective-permute-start(f32[8,1,3,66]{3,0,2,1:T(8,128)} %bitcast.1016), channel_id=1, source_target_pairs={{0,8},{8,16},{16,24},{24,32},{32,40},{40,48},{48,56},{56,64},{64,7... | collective-permute-start | bytes 19016 | tf_op jit(solution)/shard_map/ppermute | solution.py:135
  347.3 85.1 %collective-permute-start = (bf16[256,1,128]{0,2,1:T(8,128)(2,1)}, bf16[256,1,128]{0,2,1:T(8,128)(2,1)}, u32[]{:S(2)}, u32[]{:S(2)}) collective-permute-start(bf16[256,1,128]{0,2,1:T(8,128)(2,1)} %pad_maximum_fusion.8), channel_id=1, source_target_pairs={{0,128},{8,136},{16,144},{24,152},{32,160},{40,168},{48,176},{56,1... | collective-permute-start | bytes 196616 | tf_op jit(solution)/shard_map/ppermute | solution.py:88
  403.9 23.4 %collective-permute-start.81 = (f32[1,1536]{1,0:T(1,128)S(1)}, f32[1,1536]{1,0:T(1,128)S(1)}, u32[]{:S(2)}, u32[]{:S(2)}) collective-permute-start(f32[1,1536]{1,0:T(1,128)S(1)} %get-tuple-element.862), channel_id=1, source_target_pairs={{0,7},{1,0},{2,1},{3,2},{4,3},{5,4},{6,5},{7,6},{8,15},{9,8},{10,9... | collective-permute-start | bytes 18440 | tf_op jit(solution)/shard_map/ppermute | solution.py:135
  433.3 21.0 %collective-permute-start.1 = (bf16[2,256,1,128]{1,3,2,0:T(8,128)(2,1)S(1)}, bf16[2,256,1,128]{1,3,2,0:T(8,128)(2,1)S(1)}, u32[]{:S(2)}, u32[]{:S(2)}) collective-permute-start(bf16[2,256,1,128]{1,3,2,0:T(8,128)(2,1)S(1)} %pad_maximum_fusion.6), channel_id=1, source_target_pairs={{0,64},{8,72},{16,80},{24,88},{32,96},{40,104},{48,112},{56,120},{... | collective-permute-start | bytes 393224 | tf_op jit(solution)/shard_map/ppermute | solution.py:88
  473.0 25.4 %collective-permute-start.3 = (bf16[2,2,2,256,1,128]{3,5,0,1,4,2:T(8,128)(2,1)S(1)}, bf16[2,2,2,256,1,128]{3,5,0,1,4,2:T(8,128)(2,1)S(1)}, u32[]{:S(2)}, u32[]{:S(2)}) collective-permute-start(bf16[2,2,2,256,1,128]{3,5,0,1,4,2:T(8,128)(2,1)S(1)} %pad_maximum_fusion.3), channel_id=1, source_target_pairs={{0,16},{8,24},{16,0},{24,8},{32,48},{40,56},{48,32},{56,40},{64,80... | collective-permute-start | bytes 1572872 | tf_op jit(solution)/shard_map/ppermute | solution.py:88
  498.5 35.2 %collective-permute-start.4 = (bf16[2,2,2,2,256,1,128]{4,6,0,1,2,5,3:T(8,128)(2,1)S(1)}, bf16[2,2,2,2,256,1,128]{4,6,0,1,2,5,3:T(8,128)(2,1)S(1)}, u32[]{:S(2)}, u32[]{:S(2)}) collective-permute-start(bf16[2,2,2,2,256,1,128]{4,6,0,1,2,5,3:T(8,128)(2,1)S(1)} %pad_maximum_fusion.1), channel_id=1, source_target_pairs={{0,8},{8,0},{16,24},{24,16},{32,40},{40,32},{48,56},{56,48},{64,72... | collective-permute-start | bytes 3145736 | tf_op jit(solution)/shard_map/ppermute | solution.py:88
  598.9 67.6 %collective-permute-start.5 = (bf16[32,1536]{1,0:T(8,128)(2,1)S(1)}, bf16[32,1536]{1,0:T(8,128)(2,1)S(1)}, u32[]{:S(2)}, u32[]{:S(2)}) collective-permute-start(bf16[32,1536]{1,0:T(8,128)(2,1)S(1)} %get-tuple-element.845), channel_id=1, source_target_pairs={{0,7},{1,0},{2,1},{3,2},{4,3},{5,4},{6,5},{7,6},{8,15},{9,8},{10,9... | collective-permute-start | bytes 294920 | tf_op jit(solution)/shard_map/ppermute | solution.py:135
  710.4 20.9 %collective-permute-start.98 = (bf16[1,18,1536]{2,1,0:T(8,128)(2,1)S(1)}, bf16[1,18,1536]{2,1,0:T(8,128)(2,1)S(1)}, u32[]{:S(2)}, u32[]{:S(2)}) collective-permute-start(bf16[1,18,1536]{2,1,0:T(8,128)(2,1)S(1)} %get-tuple-element.758), channel_id=1, source_target_pairs={{0,168},{8,176},{16,184},{24,192},{32,200},{40,208},{48,216},{56,2... | collective-permute-start | bytes 165896 | tf_op jit(solution)/shard_map/ppermute | solution.py:135
  724.1 20.9 %collective-permute-start.102 = (bf16[1,18,1536]{2,1,0:T(8,128)(2,1)S(1)}, bf16[1,18,1536]{2,1,0:T(8,128)(2,1)S(1)}, u32[]{:S(2)}, u32[]{:S(2)}) collective-permute-start(bf16[1,18,1536]{2,1,0:T(8,128)(2,1)S(1)} %get-tuple-element.754), channel_id=1, source_target_pairs={{0,136},{8,144},{16,152},{24,160},{32,168},{40,176},{48,184},{56,1... | collective-permute-start | bytes 165896 | tf_op jit(solution)/shard_map/ppermute | solution.py:135
  737.5 22.5 %collective-permute-start.105 = (bf16[1,18,1536]{2,1,0:T(8,128)(2,1)S(1)}, bf16[1,18,1536]{2,1,0:T(8,128)(2,1)S(1)}, u32[]{:S(2)}, u32[]{:S(2)}) collective-permute-start(bf16[1,18,1536]{2,1,0:T(8,128)(2,1)S(1)} %get-tuple-element.751), channel_id=1, source_target_pairs={{0,112},{8,120},{16,128},{24,136},{32,144},{40,152},{48,160},{56,1... | collective-permute-start | bytes 165896 | tf_op jit(solution)/shard_map/ppermute | solution.py:135
  819.2 20.2 %collective-permute-start.129 = (bf16[1,18,1536]{2,1,0:T(8,128)(2,1)S(1)}, bf16[1,18,1536]{2,1,0:T(8,128)(2,1)S(1)}, u32[]{:S(2)}, u32[]{:S(2)}) collective-permute-start(bf16[1,18,1536]{2,1,0:T(8,128)(2,1)S(1)} %bitcast.962), channel_id=1, source_target_pairs={{0,168},{8,176},{16,184},{24,192},{32,200},{40,208},{48,216},{56,2... | collective-permute-start | bytes 165896 | tf_op jit(solution)/shard_map/ppermute | solution.py:135
  826.1 20.6 %collective-permute-start.131 = (bf16[1,18,1536]{2,1,0:T(8,128)(2,1)S(1)}, bf16[1,18,1536]{2,1,0:T(8,128)(2,1)S(1)}, u32[]{:S(2)}, u32[]{:S(2)}) collective-permute-start(bf16[1,18,1536]{2,1,0:T(8,128)(2,1)S(1)} %bitcast.960), channel_id=1, source_target_pairs={{0,152},{8,160},{16,168},{24,176},{32,184},{40,192},{48,200},{56,2... | collective-permute-start | bytes 165896 | tf_op jit(solution)/shard_map/ppermute | solution.py:135
  827.3 22.0 %collective-permute-start.132 = (bf16[1,18,1536]{2,1,0:T(8,128)(2,1)S(1)}, bf16[1,18,1536]{2,1,0:T(8,128)(2,1)S(1)}, u32[]{:S(2)}, u32[]{:S(2)}) collective-permute-start(bf16[1,18,1536]{2,1,0:T(8,128)(2,1)S(1)} %bitcast.959), channel_id=1, source_target_pairs={{0,144},{8,152},{16,160},{24,168},{32,176},{40,184},{48,192},{56,2... | collective-permute-start | bytes 165896 | tf_op jit(solution)/shard_map/ppermute | solution.py:135
  833.3 22.0 %collective-permute-start.133 = (bf16[1,18,1536]{2,1,0:T(8,128)(2,1)S(1)}, bf16[1,18,1536]{2,1,0:T(8,128)(2,1)S(1)}, u32[]{:S(2)}, u32[]{:S(2)}) collective-permute-start(bf16[1,18,1536]{2,1,0:T(8,128)(2,1)S(1)} %bitcast.958), channel_id=1, source_target_pairs={{0,136},{8,144},{16,152},{24,160},{32,168},{40,176},{48,184},{56,1... | collective-permute-start | bytes 165896 | tf_op jit(solution)/shard_map/ppermute | solution.py:135
  (128 other events, 2680.8 us)

commit v3 on v2

--- a/solution.py
+++ b/solution.py
@@ -123,36 +123,6 @@
         stacked = combine(keep, received)
         remaining.pop(place)
     return stacked
-
-
-def exchange_all(chunks, axis_name):
-    count = lax.axis_size(axis_name)
-    index = lax.axis_index(axis_name)
-    pieces = [lax.dynamic_index_in_dim(chunks, index, 0, keepdims=False)]
-    for shift in range(1, count):
-        outgoing = lax.dynamic_index_in_dim(chunks, (index - shift) % count, 0, keepdims=False)
-        pairs = [(i, (i - shift) % count) for i in range(count)]
-        pieces.append(lax.ppermute(outgoing, axis_name, pairs))
-    return jnp.roll(jnp.stack(pieces), index, axis=0)
-
-
-def gather_direct(block, axis_name):
-    count = lax.axis_size(axis_name)
-    index = lax.axis_index(axis_name)
-    pieces = [block]
-    for shift in range(1, count):
-        pairs = [(i, (i - shift) % count) for i in range(count)]
-        pieces.append(lax.ppermute(block, axis_name, pairs))
-    gathered = jnp.roll(jnp.stack(pieces), index, axis=0)
-    return gathered.reshape((-1,) + block.shape[1:])
-
-
-def scatter_direct(values, axis_name, send_type=None):
-    count = lax.axis_size(axis_name)
-    chunks = values.reshape((count, values.shape[0] // count) + values.shape[1:])
-    if send_type is not None:
-        chunks = chunks.astype(send_type)
-    return exchange_all(chunks, axis_name).astype(values.dtype)
 
 
 def add_parts(first, second):
@@ -281,8 +251,11 @@
         .reshape(pre_local, heads_q * head_dim)
     )
     prefill_part = jnp.dot(attended, output_weight, preferred_element_type=jnp.float32)
-    prefill_sum = jnp.sum(scatter_direct(prefill_part, "tp", send_type=jnp.bfloat16), axis=0)
-    group_states = gather_direct(decode_states, "tp")
+    tp_near_first = [1 << j for j in range(tp_count.bit_length() - 1)]
+    prefill_sum = scatter_blocks(
+        prefill_part, "tp", tp_near_first, add_parts, send_type=jnp.bfloat16
+    )
+    group_states = gather_blocks(decode_states, "tp", tp_near_first[::-1])
     group_rows = group_states.shape[0]
     group_lengths = lax.dynamic_slice_in_dim(cached_length, seq_index * group_rows, group_rows, 0)
     decode_normalised = rms_norm(group_states, attn_gain)
@@ -301,7 +274,7 @@
     ).reshape(group_rows, heads_kv, 2 * head_dim)
     new_keys = apply_rotary(decode_keyvalues[..., :head_dim], group_lengths).astype(jnp.bfloat16)
     new_vals = decode_keyvalues[..., head_dim:].astype(jnp.bfloat16)
-    decode_queries = gather_direct(group_queries, "seq")
+    decode_queries = gather_blocks(group_queries, "seq", seq_near_first[::-1])
     cache_local = cache_keyval.shape[1]
     cache_pos = seq_index * cache_local + jnp.arange(cache_local, dtype=jnp.int32)
     visible = (cache_pos[None, :] < cached_length[:, None])[:, None, None, :]
@@ -325,11 +298,8 @@
         preferred_element_type=jnp.float32,
     )
     packed = jnp.concatenate([local_acc, local_total[..., None], local_max[..., None]], axis=-1)
-    parts = scatter_direct(packed, "seq")
-    part_max = parts[..., -1]
-    merged_max = jnp.max(part_max, axis=0)
-    part_scale = jnp.exp(part_max - merged_max[None])
-    merged = jnp.sum(parts[..., :-1] * part_scale[..., None], axis=0)
+    merged = scatter_blocks(packed, "seq", seq_near_first, merge_softmax)
+    merged_max = merged[..., head_dim + 1]
     merged_acc = merged[..., :head_dim]
     merged_total = merged[..., head_dim]
     own_score = (
@@ -354,7 +324,7 @@
         .reshape(group_rows, heads_q * head_dim)
     )
     decode_part = jnp.dot(decode_attended, output_weight, preferred_element_type=jnp.float32)
-    decode_sum = jnp.sum(scatter_direct(decode_part, "tp"), axis=0)
+    decode_sum = scatter_blocks(decode_part, "tp", tp_near_first, add_parts)
     own_states = lax.dynamic_slice_in_dim(prefill_states, tp_index * pre_share, pre_share, 0)
     prefill_h = (own_states.astype(jnp.float32) + prefill_sum).astype(jnp.bfloat16)
     decode_h = (decode_states.astype(jnp.float32) + decode_sum).astype(jnp.bfloat16)
@@ -372,7 +342,7 @@
     outgoing = buffer.reshape(seq_count, EXPERTS // seq_count, capacity, model_width)
     hidden = jnp.einsum(
         "secd,edf->secf",
-        exchange_all(outgoing, "seq"),
+        lax.all_to_all(outgoing, "seq", split_axis=0, concat_axis=0, tiled=True),
         expert_in,
         preferred_element_type=jnp.float32,
     )
@@ -381,7 +351,7 @@
     results = jnp.einsum(
         "secf,efd->secd", active, expert_out, preferred_element_type=jnp.float32
     ).astype(jnp.bfloat16)
-    returned = exchange_all(results, "seq")
+    returned = lax.all_to_all(results, "seq", split_axis=0, concat_axis=0, tiled=True)
     fetched = (
         returned.reshape(EXPERTS * capacity, model_width)[slot_index]
         .astype(jnp.float32)

time: 928 us -> 440 us (0.47); the launches traced: 911 us -> 437 us
  starting transfers between devices: 504 us -> 36.5 us
  local copies, waits for them, and re-layouts: 213 us -> 71.5 us
  blocking collectives: 0 us -> 91.9 us
  waiting for transfers between devices: 96.1 us -> 127 us
  other arithmetic: 48.4 us -> 66.6 us
    ppermute x145 -> x0, starting transfers between devices: 457 us -> none  [the longest x107 346 us: exchange_all(): pieces.append(lax.ppermute(outgoing, axis_name, pairs))]
    all_to_all x0 -> x1, blocking collectives: none -> 91.9 us  [shards(): lax.all_to_all(outgoing, 'seq', split_axis=0, concat_axis=0, tiled=True)]
    dynamic_slice x33 -> x0, local copies, waits for them, and re-layouts: 75.6 us -> none  [exchange_all(): lax.dynamic_index_in_dim(chunks, (index - shift) % count, 0, keepdims=False)]
    all_to_all x0 -> x1, waiting for transfers between devices: none -> 53.8 us  [shards(): lax.all_to_all(results, 'seq', split_axis=0, concat_axis=0, tiled=True)]
    another operation x38 -> x0, local copies, waits for them, and re-layouts: 50.4 us -> none  [the longest x33 44.5 us: exchange_all(): return jnp.roll(jnp.stack(pieces), index, axis=0)]
    concatenate x5 -> x0, local copies, waits for them, and re-layouts: 40.3 us -> none  [the longest x3 38.6 us: exchange_all(): return jnp.roll(jnp.stack(pieces), index, axis=0)]
    ppermute x145 -> x0, waiting for transfers between devices: 40.2 us -> none  [the longest x107 35.9 us: exchange_all(): pieces.append(lax.ppermute(outgoing, axis_name, pairs))]
    ppermute x5 -> x24, waiting for transfers between devices: 55.9 us -> 73.1 us  [swap_partner(): return lax.ppermute(values, axis_name, pairs)]
  transfers between devices with their start and end apart: 150 -> 25, of which waited for: 27 -> 17; matrix products, arithmetic and copies ran while one was open for 20% -> 23% of each run, Pallas kernels for 0% -> 0%
where the time goes in v3:
time: 440 us; the launch traced here: 437 us
  waiting for transfers between devices  127 us (29%)
  blocking collectives  91.9 us (21%)
  local copies, waits for them, and re-layouts  71.5 us (16%)
  other arithmetic  66.6 us (15%)
  starting transfers between devices  36.5 us (8%)
  loops' own time  21.3 us (5%)
  matrix products  20.3 us (5%)
    all_to_all x1, blocking collectives, shards(): lax.all_to_all(outgoing, 'seq', split_axis=0, concat_axis=0, tiled=True)  91.9 us
    ppermute x24, waiting for transfers between devices, swap_partner(): return lax.ppermute(values, axis_name, pairs)  73.1 us
    all_to_all x1, waiting for transfers between devices, shards(): lax.all_to_all(results, 'seq', split_axis=0, concat_axis=0, tiled=True)  53.8 us
    ppermute x24, starting transfers between devices, swap_partner(): return lax.ppermute(values, axis_name, pairs)  30 us
    another operation x1, loops' own time, shards(): lax.scan(one_block, start_state, (jnp.arange(piece_rows // block_len, dty...  21 us
    dynamic_slice x16, local copies, waits for them, and re-layouts, shards(): lax.scan(one_block, start_state, (jnp.arange(piece_rows // block_len, dty...  20.9 us
    reduce_or x16, other arithmetic, one_block(): jnp.any(token_visible)  15 us
    another operation x33, other arithmetic, gather_blocks(): stacked = jnp.stack([low, high], axis=place)  14.3 us
  transfers between devices with their start and end apart: 25, of which 17 were waited for; matrix products, arithmetic and copies ran while one was open for 23% of the time, Pallas kernels for 0%

profile of v3, /device:TPU:10, one launch (start us, length us, event | category | flops | bytes accessed | tf_op | source)
XLA Modules:
  0.0 437.2 jit_solution(12356114720461942081)
XLA Ops:
  5.6 1.7 convolution_bitcast_fusion.1
  8.2 7.2 %collective-permute-start = (bf16[256,1,128]{0,2,1:T(8,128)(2,1)}, bf16[256,1,128]{0,2,1:T(8,128)(2,1)}, u32[]{:S(2)}, u32[]{:S(2)}) collective-permute-start(bf16[256,1,128]{0,2,1:T(8,128)(2,1)} %pad_maximum_fusion.11), channel_id=1, source_target_pairs={{0,128},{8,136},{16,144},{24,152},{32,160},{40,168},{48,176},{56,1... | collective-permute-start | bytes 196616 | tf_op jit(solution)/shard_map/ppermute | solution.py:88
  15.4 2.3 collective-permute-start.8
  19.5 1.8 fusion.75
  26.3 2.2 subtract_convert_fusion
  31.4 1.8 concatenate.97
  34.2 1.8 pad_maximum_fusion.5
  40.9 6.7 %collective-permute-done.11 = bf16[8,1,3,64]{3,0,2,1:T(8,128)(2,1)S(1)} collective-permute-done((bf16[8,1,3,64]{3,0,2,1:T(8,128)(2,1)S(1)}, bf16[8,1,3,64]{3,0,2,1:T(8,128)(2,1)S(1)}, u32[]{:S(2)}, u32[]{:S(2)}) %collective-permute-start.11) | collective-permute-done | bytes 3104 | tf_op jit(solution)/shard_map/ppermute | solution.py:88
  47.6 1.6 collective-permute-start.12
  49.8 2.5 collective-permute-done.12
  54.1 2.1 collective-permute-done.13
  56.3 2.2 collective-permute-start.14
  59.4 3.0 collective-permute-done.14
  63.4 1.6 collective-permute-start.1
  65.0 2.2 collective-permute-done.15
  67.3 4.7 %fusion.162 = (f32[256,3]{1,0:T(8,128)S(1)}, f32[256,3,64]{2,1,0:T(4,128)S(1)}) fusion(bf16[256,64,1,128]{3,1,0,2:T(8,128)(2,1)} %bitcast.431, bf16[256,3,64]{2,0,1:T(8,128)(2,1)S(1)} %bitcast.421, pred[256,64]{1,0:T(8,128)(4,1)S(1)} %copy-done.27), kind=kOutput, calls=%fused_computation.346 | convolution fusion | flops 6438144 | bytes 4508672 | tf_op jit(solution)/shard_map/bhgd,bkhd->bhgk/dot_general | solution.py:282
  72.1 1.7 fusion.22
  75.2 3.3 copy.751
  78.5 3.3 copy.752
  84.4 4.6 %collective-permute-done.16 = f32[2,2,2,2,8,1,3,66]{7,4,6,5,3,2,1,0:T(8,128)S(1)} collective-permute-done((f32[2,2,2,2,8,1,3,66]{7,4,6,5,3,2,1,0:T(8,128)S(1)}, f32[2,2,2,2,8,1,3,66]{7,4,6,5,3,2,1,0:T(8,128)S(1)}, u32[]{:S(2)}, u32[]{:S(2)}) %collective-permute-start.16) | collective-permute-done | bytes 101408 | tf_op jit(solution)/shard_map/ppermute | solution.py:88
  92.0 1.9 copy.755
  96.0 1.9 collective-permute-start.17
  98.0 4.1 collective-permute-done.17
  108.3 3.0 collective-permute-done.18
  114.8 1.5 collective-permute-start.19
  116.3 3.2 collective-permute-done.19
  122.7 6.4 %collective-permute-done.20 = f32[8,1,3,66]{3,0,2,1:T(8,128)S(1)} collective-permute-done((f32[8,1,3,66]{3,0,2,1:T(8,128)S(1)}, f32[8,1,3,66]{3,0,2,1:T(8,128)S(1)}, u32[]{:S(2)}, u32[]{:S(2)}) %collective-permute-start.20) | collective-permute-done | bytes 6368 | tf_op jit(solution)/shard_map/ppermute | solution.py:88
  133.0 1.9 collective-permute-start.3
  136.4 11.5 %collective-permute-done.3 = bf16[2,2,2,256,1,128]{3,5,0,1,2,4:T(8,128)(2,1)} collective-permute-done((bf16[2,2,2,256,1,128]{3,5,0,1,2,4:T(8,128)(2,1)}, bf16[2,2,2,256,1,128]{3,5,0,1,2,4:T(8,128)(2,1)}, u32[]{:S(2)}, u32[]{:S(2)}) %collective-permute-start.3) | collective-permute-done | bytes 524320 | tf_op jit(solution)/shard_map/ppermute | solution.py:88
  155.2 11.5 %collective-permute-done.4 = bf16[2,2,2,2,256,1,128]{4,6,0,1,2,3,5:T(8,128)(2,1)} collective-permute-done((bf16[2,2,2,2,256,1,128]{4,6,0,1,2,3,5:T(8,128)(2,1)}, bf16[2,2,2,2,256,1,128]{4,6,0,1,2,3,5:T(8,128)(2,1)}, u32[]{:S(2)}, u32[]{:S(2)}) %collective-permute-start.4) | collective-permute-done | bytes 1048608 | tf_op jit(solution)/shard_map/ppermute | solution.py:88
  166.7 1.7 select_bitcast_fusion
  169.8 1.5 pad_maximum_fusion
  171.3 4.2 copy.711
  176.0 63.0 %while.18 = (s32[]{:T(128)}, f32[1,768]{1,0:T(1,128)S(1)}, f32[1,768]{1,0:T(1,128)S(1)}, f32[1,768,64]{1,2,0:T(8,128)S(1)}, s32[256]{0:T(256)S(1)}, /*index=5*/s...) while((s32[]{:T(128)}, f32[1,768]{1,0:T(1,128)S(1)}, ...), condition=%wide.region_11.12_spmd.clone.clone, body=%wide.region_4.11_spmd.clone.clone.sunk | while | flops 108380672 | bytes 5859659 | solution.py:243
  179.7 4.1 conditional.4
  242.6 1.7 collective-permute-done.5
  246.5 5.0 %collective-permute-done.6 = bf16[2,32,1536]{2,1,0:T(8,128)(2,1)S(1)} collective-permute-done((bf16[2,32,1536]{2,1,0:T(8,128)(2,1)S(1)}, bf16[2,32,1536]{2,1,0:T(8,128)(2,1)S(1)}, u32[]{:S(2)}, u32[]{:S(2)}) %collective-permute-start.6) | collective-permute-done | bytes 196640 | tf_op jit(solution)/shard_map/ppermute | solution.py:88
  252.7 5.1 %collective-permute-done.7 = bf16[32,1536]{1,0:T(8,128)(2,1)S(1)} collective-permute-done((bf16[32,1536]{1,0:T(8,128)(2,1)S(1)}, bf16[32,1536]{1,0:T(8,128)(2,1)S(1)}, u32[]{:S(2)}, u32[]{:S(2)}) %collective-permute-start.7) | collective-permute-done | bytes 98336 | tf_op jit(solution)/shard_map/ppermute | solution.py:88
  259.0 3.3 scatter_custom_fusion
  262.3 3.6 reshape.1334
  265.9 91.9 %all_to_all.10 = bf16[32,1,18,1536]{3,2,1,0:T(8,128)(2,1)S(1)} all-to-all(bf16[32,1,18,1536]{3,2,1,0:T(8,128)(2,1)} %bitcast.410), channel_id=1, replica_groups=mesh['seq'=32,'tp'=8] {'seq'}, dimensions={0} | all-to-all | bytes 3538944 | tf_op jit(solution)/shard_map/all_to_all | solution.py:345
  357.9 2.0 fusion.29
  361.0 2.4 copy.797
  363.4 6.5 %all-to-all-start.1 = ((bf16[32,1,18,1536]{3,2,1,0:T(8,128)(2,1)}), bf16[32,1,18,1536]{3,2,1,0:T(8,128)(2,1)}, u32[]{:S(2)}, u32[]{:S(2)}) async-start(bf16[32,1,18,1536]{3,2,1,0:T(8,128)(2,1)} %copy.797), calls=%async_computation.1 | async-start | bytes 4718592 | tf_op jit(solution)/shard_map/all_to_all | solution.py:354
  370.1 53.8 %all-to-all-done.1 = bf16[32,1,18,1536]{3,2,1,0:T(8,128)(2,1)} async-done(((bf16[32,1,18,1536]{3,2,1,0:T(8,128)(2,1)}), bf16[32,1,18,1536]{3,2,1,0:T(8,128)(2,1)}, u32[]{:S(2)}, u32[]{:S(2)}) %all-to-all-start.1) | async-done | bytes 1769504 | tf_op jit(solution)/shard_map/all_to_all | solution.py:354
  423.8 3.8 reshape.1339
  427.7 5.8 %gather_fusion = bf16[264,1536]{1,0:T(8,128)(2,1)} fusion(bf16[576,1536]{1,0:T(8,128)(2,1)} %reshape.1339, s32[1024]{0:T(1024)S(1)} %pad_clamp_fusion), kind=kCustom, calls=%fused_computation | custom fusion | bytes 1623072 | tf_op jit(solution)/shard_map/gather | solution.py:356
  433.5 2.0 fusion.34
  (419 shorter events, 114.4 us)
Async XLA Ops:
  0.6 357.3 %copy-start = (bf16[1,1536,1024]{2,1,0:T(8,128)(2,1)S(1)}, bf16[1,1536,1024]{2,1,0:T(8,128)(2,1)}, u32[]{:S(2)}) copy-start(bf16[1,1536,1024]{2,1,0:T(8,128)(2,1)} %param.28) | copy-start | bytes 9437188
  0.6 18.2 %copy-start.39 = (s32[33,8]{0,1:T(8,128)S(1)}, s32[33,8]{0,1:T(8,128)}, u32[]{:S(2)}) copy-start(s32[33,8]{0,1:T(8,128)} %param.30) | copy-start | bytes 3172
  0.7 22.8 %copy-start.43 = (f32[32]{0:T(128)}, f32[32]{0:T(128)S(1)}, u32[]{:S(2)}) copy-start(f32[32]{0:T(128)S(1)} %multiply_power_fusion) | copy-start | bytes 388
  4.2 17.2 %copy-start.31 = (f32[1536]{0:T(1024)}, f32[1536]{0:T(1024)S(1)}, u32[]{:S(2)}) copy-start(f32[1536]{0:T(1024)S(1)} %convert_element_type.238) | copy-start | bytes 18436
  7.5 10.1 %copy-start.25 = (bf16[256,1,32]{0,2,1:T(8,128)(2,1)}, bf16[256,1,32]{0,2,1:T(8,128)(2,1)S(1)}, u32[]{:S(2)}) copy-start(bf16[256,1,32]{0,2,1:T(8,128)(2,1)S(1)} %get-tuple-element.436) | copy-start | bytes 49156
  8.2 50.3 %collective-permute-start = (bf16[256,1,128]{0,2,1:T(8,128)(2,1)}, bf16[256,1,128]{0,2,1:T(8,128)(2,1)}, u32[]{:S(2)}, u32[]{:S(2)}) collective-permute-start(bf16[256,1,128]{0,2,1:T(8,128)(2,1)} %pad_maximum_fusion.11), channel_id=1, source_target_pairs={{0,128},{8,136},{16,144},{24,152},{32,160},{40,168},{48,176},{56,1... | collective-permute-start | bytes 196616 | tf_op jit(solution)/shard_map/ppermute | solution.py:88
  15.4 13.2 %collective-permute-start.8 = (bf16[1,1536]{1,0:T(2,128)(2,1)}, bf16[1,1536]{1,0:T(2,128)(2,1)}, u32[]{:S(2)}, u32[]{:S(2)}) collective-permute-start(bf16[1,1536]{1,0:T(2,128)(2,1)} %param.19), channel_id=1, source_target_pairs={{0,4},{1,5},{2,6},{3,7},{4,0},{5,1},{6,2},{7,3},{8,12},{9,13},{10,... | collective-permute-start | bytes 9224 | tf_op jit(solution)/shard_map/ppermute | solution.py:88
  28.5 9.0 %copy-start.44 = (f32[32]{0:T(128)S(1)}, f32[32]{0:T(128)}, u32[]{:S(2)}) copy-start(f32[32]{0:T(128)} %copy-done.43) | copy-start | bytes 388
  28.5 11.2 %copy-start.41 = (f32[8,32]{1,0:T(8,128)S(1)}, f32[8,32]{1,0:T(8,128)}, u32[]{:S(2)}) copy-start(f32[8,32]{1,0:T(8,128)} %get-tuple-element.453) | copy-start | bytes 3076
  28.5 11.2 %copy-start.42 = (f32[8,32]{1,0:T(8,128)S(1)}, f32[8,32]{1,0:T(8,128)}, u32[]{:S(2)}) copy-start(f32[8,32]{1,0:T(8,128)} %get-tuple-element.454) | copy-start | bytes 3076
  29.3 4.7 %collective-permute-start.9 = (bf16[2,1,1536]{2,0,1:T(2,128)(2,1)S(1)}, bf16[2,1,1536]{2,0,1:T(2,128)(2,1)S(1)}, u32[]{:S(2)}, u32[]{:S(2)}) collective-permute-start(bf16[2,1,1536]{2,0,1:T(2,128)(2,1)S(1)} %pad_maximum_fusion.20), channel_id=1, source_target_pairs={{0,2},{1,3},{2,0},{3,1},{4,6},{5,7},{6,4},{7,5},{8,10},{9,11},{10,... | collective-permute-start | bytes 18440 | tf_op jit(solution)/shard_map/ppermute | solution.py:88
  31.4 8.8 %copy-start.40 = (s32[33,8]{0,1:T(8,128)S(1)}, s32[33,8]{0,1:T(8,128)}, u32[]{:S(2)}) copy-start(s32[33,8]{0,1:T(8,128)} %broadcast_multiply_fusion) | copy-start | bytes 3172
  33.2 25.3 %copy-start.22 = (bf16[256,1,64]{0,2,1:T(8,128)(2,1)S(1)}, bf16[256,1,64]{0,2,1:T(8,128)(2,1)}, u32[]{:S(2)}) copy-start(bf16[256,1,64]{0,2,1:T(8,128)(2,1)} %copy-done.21) | copy-start | bytes 98308
  33.2 25.3 %copy-start.26 = (bf16[256,1,32]{0,2,1:T(8,128)(2,1)S(1)}, bf16[256,1,32]{0,2,1:T(8,128)(2,1)}, u32[]{:S(2)}) copy-start(bf16[256,1,32]{0,2,1:T(8,128)(2,1)} %copy-done.25) | copy-start | bytes 49156
  34.1 1.9 collective-permute-start.10
  39.7 27.7 %copy-start.27 = (pred[256,64]{1,0:T(8,128)(4,1)S(1)}, pred[256,64]{1,0:T(8,128)(4,1)}, u32[]{:S(2)}) copy-start(pred[256,64]{1,0:T(8,128)(4,1)} %broadcast_compare_fusion) | copy-start | bytes 49156
  40.0 32.0 %copy-start.33 = (f32[8,3]{0,1:T(4,128)}, f32[8,3]{0,1:T(4,128)S(1)}, u32[]{:S(2)}) copy-start(f32[8,3]{0,1:T(4,128)S(1)} %get-tuple-element.406) | copy-start | bytes 292
  40.0 7.6 %collective-permute-start.11 = (bf16[8,1,3,64]{3,0,2,1:T(8,128)(2,1)S(1)}, bf16[8,1,3,64]{3,0,2,1:T(8,128)(2,1)S(1)}, u32[]{:S(2)}, u32[]{:S(2)}) collective-permute-start(bf16[8,1,3,64]{3,0,2,1:T(8,128)(2,1)S(1)} %get-tuple-element.407), channel_id=1, source_target_pairs={{0,128},{8,136},{16,144},{24,152},{32,160},{40,168},{48,176},{56,1... | collective-permute-start | bytes 9224 | tf_op jit(solution)/shard_map/ppermute | solution.py:88
  47.6 4.7 %collective-permute-start.12 = (bf16[2,8,1,3,64]{4,1,3,0,2:T(8,128)(2,1)S(1)}, bf16[2,8,1,3,64]{4,1,3,0,2:T(8,128)(2,1)S(1)}, u32[]{:S(2)}, u32[]{:S(2)}) collective-permute-start(bf16[2,8,1,3,64]{4,1,3,0,2:T(8,128)(2,1)S(1)} %fusion.128), channel_id=1, source_target_pairs={{0,64},{8,72},{16,80},{24,88},{32,96},{40,104},{48,112},{56,120},{... | collective-permute-start | bytes 18440 | tf_op jit(solution)/shard_map/ppermute | solution.py:88
  52.3 3.9 collective-permute-start.13
  56.3 6.1 %collective-permute-start.14 = (bf16[2,2,2,8,1,3,64]{6,3,5,0,1,2,4:T(8,128)(2,1)S(1)}, bf16[2,2,2,8,1,3,64]{6,3,5,0,1,2,4:T(8,128)(2,1)S(1)}, u32[]{:S(2)}, u32[]{:S(2)}) collective-permute-start(bf16[2,2,2,8,1,3,64]{6,3,5,0,1,2,4:T(8,128)(2,1)S(1)} %fusion.105), channel_id=1, source_target_pairs={{0,16},{8,24},{16,0},{24,8},{32,48},{40,56},{48,32},{56,40},{64,80... | collective-permute-start | bytes 73736 | tf_op jit(solution)/shard_map/ppermute | solution.py:88
  62.5 4.7 %collective-permute-start.15 = (bf16[2,2,2,2,8,1,3,64]{7,4,6,0,1,2,3,5:T(8,128)(2,1)S(1)}, bf16[2,2,2,2,8,1,3,64]{7,4,6,0,1,2,3,5:T(8,128)(2,1)S(1)}, u32[]{:S(2)}, u32[]{:S(2)}) collective-permute-start(bf16[2,2,2,2,8,1,3,64]{7,4,6,0,1,2,3,5:T(8,128)(2,1)S(1)} %fusion.89), channel_id=1, source_target_pairs={{0,8},{8,0},{16,24},{24,16},{32,40},{40,32},{48,56},{56,48},{64,72... | collective-permute-start | bytes 147464 | tf_op jit(solution)/shard_map/ppermute | solution.py:88
  63.4 20.1 %collective-permute-start.1 = (bf16[2,256,1,128]{1,3,0,2:T(8,128)(2,1)}, bf16[2,256,1,128]{1,3,0,2:T(8,128)(2,1)}, u32[]{:S(2)}, u32[]{:S(2)}) collective-permute-start(bf16[2,256,1,128]{1,3,0,2:T(8,128)(2,1)} %fusion.88), channel_id=1, source_target_pairs={{0,64},{8,72},{16,80},{24,88},{32,96},{40,104},{48,112},{56,120},{... | collective-permute-start | bytes 393224 | tf_op jit(solution)/shard_map/ppermute | solution.py:88
  83.2 5.8 %collective-permute-start.16 = (f32[2,2,2,2,8,1,3,66]{7,4,6,5,3,2,1,0:T(8,128)S(1)}, f32[2,2,2,2,8,1,3,66]{7,4,6,5,3,2,1,0:T(8,128)S(1)}, u32[]{:S(2)}, u32[]{:S(2)}) collective-permute-start(f32[2,2,2,2,8,1,3,66]{7,4,6,5,3,2,1,0:T(8,128)S(1)} %copy.753), channel_id=1, source_target_pairs={{0,8},{8,0},{16,24},{24,16},{32,40},{40,32},{48,56},{56,48},{64,72... | collective-permute-start | bytes 304136 | tf_op jit(solution)/shard_map/ppermute | solution.py:88
  96.0 6.2 %collective-permute-start.17 = (f32[2,2,2,8,1,3,66]{6,3,5,4,2,1,0:T(8,128)S(1)}, f32[2,2,2,8,1,3,66]{6,3,5,4,2,1,0:T(8,128)S(1)}, u32[]{:S(2)}, u32[]{:S(2)}) collective-permute-start(f32[2,2,2,8,1,3,66]{6,3,5,4,2,1,0:T(8,128)S(1)} %copy.760), channel_id=1, source_target_pairs={{0,16},{8,24},{16,0},{24,8},{32,48},{40,56},{48,32},{56,40},{64,80... | collective-permute-start | bytes 152072 | tf_op jit(solution)/shard_map/ppermute | solution.py:88
  98.0 18.3 %copy-start.12 = (bf16[1,256,1,128]{1,3,2,0:T(8,128)(2,1)S(1)}, bf16[1,256,1,128]{1,3,2,0:T(8,128)(2,1)}, u32[]{:S(2)}) copy-start(bf16[1,256,1,128]{1,3,2,0:T(8,128)(2,1)} %copy-done.10) | copy-start | bytes 196612
  98.0 18.3 %copy-start.15 = (bf16[1,256,1,128]{1,3,2,0:T(8,128)(2,1)S(1)}, bf16[1,256,1,128]{1,3,2,0:T(8,128)(2,1)}, u32[]{:S(2)}) copy-start(bf16[1,256,1,128]{1,3,2,0:T(8,128)(2,1)} %copy-done.13) | copy-start | bytes 196612
  107.0 22.4 %copy-start.29 = (f32[8,1,3,1]{3,0,2,1:T(8,128)S(1)}, f32[8,1,3,1]{3,0,2,1:T(8,128)}, u32[]{:S(2)}) copy-start(f32[8,1,3,1]{3,0,2,1:T(8,128)} %copy.779) | copy-start | bytes 292
  107.0 22.5 %copy-start.34 = (f32[8,3]{0,1:T(4,128)S(1)}, f32[8,3]{0,1:T(4,128)}, u32[]{:S(2)}) copy-start(f32[8,3]{0,1:T(4,128)} %copy-done.33) | copy-start | bytes 292
  107.1 4.2 collective-permute-start.18
  114.8 4.8 %collective-permute-start.19 = (f32[2,8,1,3,66]{4,1,3,2,0:T(8,128)S(1)}, f32[2,8,1,3,66]{4,1,3,2,0:T(8,128)S(1)}, u32[]{:S(2)}, u32[]{:S(2)}) collective-permute-start(f32[2,8,1,3,66]{4,1,3,2,0:T(8,128)S(1)} %select_bitcast_fusion.14), channel_id=1, source_target_pairs={{0,64},{8,72},{16,80},{24,88},{32,96},{40,104},{48,112},{56,120},{... | collective-permute-start | bytes 38024 | tf_op jit(solution)/shard_map/ppermute | solution.py:88
  116.3 13.2 %copy-start.7 = (bf16[2,1,256,1,128]{2,4,0,3,1:T(8,128)(2,1)}, bf16[2,1,256,1,128]{2,4,0,3,1:T(8,128)(2,1)S(1)}, u32[]{:S(2)}) copy-start(bf16[2,1,256,1,128]{2,4,0,3,1:T(8,128)(2,1)S(1)} %select_bitcast_fusion.5) | copy-start | bytes 393220
  121.5 13.4 %copy-start.38 = (f32[8,64]{1,0:T(8,128)S(1)}, f32[8,64]{1,0:T(8,128)}, u32[]{:S(2)}) copy-start(f32[8,64]{1,0:T(8,128)} %bitcast_convert_fusion) | copy-start | bytes 6148
  121.5 7.6 %collective-permute-start.20 = (f32[8,1,3,66]{3,0,2,1:T(8,128)S(1)}, f32[8,1,3,66]{3,0,2,1:T(8,128)S(1)}, u32[]{:S(2)}, u32[]{:S(2)}) collective-permute-start(f32[8,1,3,66]{3,0,2,1:T(8,128)S(1)} %select_bitcast_fusion.17), channel_id=1, source_target_pairs={{0,128},{8,136},{16,144},{24,152},{32,160},{40,168},{48,176},{56,1... | collective-permute-start | bytes 19016 | tf_op jit(solution)/shard_map/ppermute | solution.py:88
  121.6 8.0 %collective-permute-start.2 = (bf16[2,2,256,1,128]{2,4,0,1,3:T(8,128)(2,1)S(1)}, bf16[2,2,256,1,128]{2,4,0,1,3:T(8,128)(2,1)S(1)}, u32[]{:S(2)}, u32[]{:S(2)}) collective-permute-start(bf16[2,2,256,1,128]{2,4,0,1,3:T(8,128)(2,1)S(1)} %fusion.82), channel_id=1, source_target_pairs={{0,32},{8,40},{16,48},{24,56},{32,0},{40,8},{48,16},{56,24},{64,96... | collective-permute-start | bytes 786440 | tf_op jit(solution)/shard_map/ppermute | solution.py:88
  133.0 14.9 %collective-permute-start.3 = (bf16[2,2,2,256,1,128]{3,5,0,1,2,4:T(8,128)(2,1)}, bf16[2,2,2,256,1,128]{3,5,0,1,2,4:T(8,128)(2,1)}, u32[]{:S(2)}, u32[]{:S(2)}) collective-permute-start(bf16[2,2,2,256,1,128]{3,5,0,1,2,4:T(8,128)(2,1)} %fusion.64), channel_id=1, source_target_pairs={{0,16},{8,24},{16,0},{24,8},{32,48},{40,56},{48,32},{56,40},{64,80... | collective-permute-start | bytes 1572872 | tf_op jit(solution)/shard_map/ppermute | solution.py:88
  135.1 13.8 %copy-start.6 = (bf16[2,2,1,256,1,128]{3,5,0,1,4,2:T(8,128)(2,1)S(1)}, bf16[2,2,1,256,1,128]{3,5,0,1,4,2:T(8,128)(2,1)}, u32[]{:S(2)}) copy-start(bf16[2,2,1,256,1,128]{3,5,0,1,4,2:T(8,128)(2,1)} %copy-done.5) | copy-start | bytes 786436
  151.4 15.3 %collective-permute-start.4 = (bf16[2,2,2,2,256,1,128]{4,6,0,1,2,3,5:T(8,128)(2,1)}, bf16[2,2,2,2,256,1,128]{4,6,0,1,2,3,5:T(8,128)(2,1)}, u32[]{:S(2)}, u32[]{:S(2)}) collective-permute-start(bf16[2,2,2,2,256,1,128]{4,6,0,1,2,3,5:T(8,128)(2,1)} %fusion.48), channel_id=1, source_target_pairs={{0,8},{8,0},{16,24},{24,16},{32,40},{40,32},{48,56},{56,48},{64,72... | collective-permute-start | bytes 3145736 | tf_op jit(solution)/shard_map/ppermute | solution.py:88
  152.6 1.3 collective-permute-start.21
  154.5 13.9 %copy-start.2 = (bf16[2,2,2,1,256,1,128]{4,6,0,1,2,5,3:T(8,128)(2,1)S(1)}, bf16[2,2,2,1,256,1,128]{4,6,0,1,2,5,3:T(8,128)(2,1)}, u32[]{:S(2)}) copy-start(bf16[2,2,2,1,256,1,128]{4,6,0,1,2,5,3:T(8,128)(2,1)} %copy-done.1) | copy-start | bytes 1572868
  154.5 13.9 %copy-start.4 = (bf16[2,2,2,1,256,1,128]{4,6,0,1,2,5,3:T(8,128)(2,1)S(1)}, bf16[2,2,2,1,256,1,128]{4,6,0,1,2,5,3:T(8,128)(2,1)}, u32[]{:S(2)}) copy-start(bf16[2,2,2,1,256,1,128]{4,6,0,1,2,5,3:T(8,128)(2,1)} %copy-done.3) | copy-start | bytes 1572868
  154.5 88.0 %collective-permute-start.22 = (f32[2,1,1536]{2,1,0:T(1,128)}, f32[2,1,1536]{2,1,0:T(1,128)S(1)}, u32[]{:S(2)}, u32[]{:S(2)}) collective-permute-start(f32[2,1,1536]{2,1,0:T(1,128)} %fusion.122), channel_id=1, source_target_pairs={{0,2},{1,3},{2,0},{3,1},{4,6},{5,7},{6,4},{7,5},{8,10},{9,11},{10,... | collective-permute-start | bytes 36872 | tf_op jit(solution)/shard_map/ppermute | solution.py:88
  242.4 1.8 collective-permute-start.5
  244.4 14.7 %copy-start.45 = (s32[264]{0:T(512)S(1)}, s32[264]{0:T(512)}, u32[]{:S(2)}) copy-start(s32[264]{0:T(512)} %fusion.154) | copy-start | bytes 3172
  244.4 7.1 %collective-permute-start.6 = (bf16[2,32,1536]{2,1,0:T(8,128)(2,1)S(1)}, bf16[2,32,1536]{2,1,0:T(8,128)(2,1)S(1)}, u32[]{:S(2)}, u32[]{:S(2)}) collective-permute-start(bf16[2,32,1536]{2,1,0:T(8,128)(2,1)S(1)} %fusion.78), channel_id=1, source_target_pairs={{0,2},{1,3},{2,0},{3,1},{4,6},{5,7},{6,4},{7,5},{8,10},{9,11},{10,... | collective-permute-start | bytes 589832 | tf_op jit(solution)/shard_map/ppermute | solution.py:88
  245.2 6.8 %collective-permute-start.23 = (f32[1,1536]{1,0:T(1,128)S(1)}, f32[1,1536]{1,0:T(1,128)S(1)}, u32[]{:S(2)}, u32[]{:S(2)}) collective-permute-start(f32[1,1536]{1,0:T(1,128)S(1)} %fusion.132), channel_id=1, source_target_pairs={{0,4},{1,5},{2,6},{3,7},{4,0},{5,1},{6,2},{7,3},{8,12},{9,13},{10,... | collective-permute-start | bytes 18440 | tf_op jit(solution)/shard_map/ppermute | solution.py:88
  251.6 6.2 %collective-permute-start.7 = (bf16[32,1536]{1,0:T(8,128)(2,1)S(1)}, bf16[32,1536]{1,0:T(8,128)(2,1)S(1)}, u32[]{:S(2)}, u32[]{:S(2)}) collective-permute-start(bf16[32,1536]{1,0:T(8,128)(2,1)S(1)} %fusion.85), channel_id=1, source_target_pairs={{0,4},{1,5},{2,6},{3,7},{4,0},{5,1},{6,2},{7,3},{8,12},{9,13},{10,... | collective-permute-start | bytes 294920 | tf_op jit(solution)/shard_map/ppermute | solution.py:88
  363.4 60.4 %all-to-all-start.1 = ((bf16[32,1,18,1536]{3,2,1,0:T(8,128)(2,1)}), bf16[32,1,18,1536]{3,2,1,0:T(8,128)(2,1)}, u32[]{:S(2)}, u32[]{:S(2)}) async-start(bf16[32,1,18,1536]{3,2,1,0:T(8,128)(2,1)} %copy.797), calls=%async_computation.1 | async-start | bytes 4718592 | tf_op jit(solution)/shard_map/all_to_all | solution.py:354
  (31 other events, 101.5 us)
